TPU v7x, 256 devices: a whole 4x4x8 slice. The times are simulated.
256 devices in a mesh: gx: 16 (over x, y), gy: 4 (over z_hi, core), gz: 4 (over z_lo).
Axes of the slice: x: 4, y: 4, z: 8 (z_hi: 2, z_lo: 4; z = z_hi * 4 + z_lo), core: 2. Of those that a mesh axis runs over, the one named last changes fastest.
Arguments:
- populations: float32 [19, 256, 64, 1024], P(None, 'gx', 'gy', 'gz'), may hold values from 0.01 to 0.11
- marker_force: float32 [3, 262144], P(None, ('gx', 'gy', 'gz')), may hold values from -12 to 12
- marker_offset: float32 [3, 262144], P(None, ('gx', 'gy', 'gz')), may hold values from 0 to 1
- marker_owner: int32 [262144, 1], P(('gx', 'gy', 'gz')), may hold values from 0 to 255; in each aligned block of 1024 rows (0 to 1023, 1024 to 2047, ...) at most 8 rows name the same one
- marker_cell: int32 [262144], P(('gx', 'gy', 'gz')), may hold values from 0 to 65535
Outputs:
- new_populations: float32 [19, 256, 64, 1024], P(None, 'gx', 'gy', 'gz')
- marker_velocity: float32 [3, 262144], P(None, ('gx', 'gy', 'gz'))
Inputs may be any that keep to these rules, and one draw needn't show every extreme that they name: `marker_owner`: among the 1024 markers of one device no owner is named more than 8 times, and some device names one owner exactly 8 times.
All inputs are finite; a program needn't handle non-finite values.
Results may differ from a plain program's by a relative error of at most 0.00012.
Values sent between devices are 32-bit elements; how exact they have to be, the bound alone decides.
No kernel may reach another device: no remote copies, remote signals or barrier semaphores. Data moves between devices by JAX's collectives and lax.ppermute only.
A program may use at most 128 MiB of HBM per device.

v0:
```python
import jax
import jax.numpy as jnp
from jax import lax
from jax.sharding import PartitionSpec as P

CX = 16
CY = 16
CZ = 256
MARK_DEV = 1024


lattice_speeds = (
    (0, 0, 0),
    (1, 0, 0),
    (-1, 0, 0),
    (0, 1, 0),
    (0, -1, 0),
    (0, 0, 1),
    (0, 0, -1),
    (1, 1, 0),
    (-1, -1, 0),
    (1, -1, 0),
    (-1, 1, 0),
    (1, 0, 1),
    (-1, 0, -1),
    (1, 0, -1),
    (-1, 0, 1),
    (0, 1, 1),
    (0, -1, -1),
    (0, 1, -1),
    (0, -1, 1),
)
lattice_weights = (1.0 / 3.0,) + (1.0 / 18.0,) * 6 + (1.0 / 36.0,) * 12
relaxation = 0.8
highest = lax.Precision.HIGHEST
three_pass = lax.Precision.HIGH


def extended_2(cells, sides, width):
    for axis, dim in sides:
        count = lax.axis_size(axis)
        head = lax.slice_in_dim(cells, 0, width, axis=dim)
        tail = lax.slice_in_dim(cells, cells.shape[dim] - width, cells.shape[dim], axis=dim)
        cells = jnp.concatenate(
            [
                lax.ppermute(tail, axis, [(i, (i + 1) % count) for i in range(count)]),
                cells,
                lax.ppermute(head, axis, [((i + 1) % count, i) for i in range(count)]),
            ],
            axis=dim,
        )
    return cells


def pass_axis(fields, axis, dim):
    count = lax.axis_size(axis)
    extent = fields[0].shape[dim]
    up = [i for i in range(len(fields)) if lattice_speeds[i][dim] == 1]
    down = [i for i in range(len(fields)) if lattice_speeds[i][dim] == -1]
    going_up = jnp.stack([lax.slice_in_dim(fields[i], extent - 1, extent, axis=dim) for i in up])
    going_down = jnp.stack([lax.slice_in_dim(fields[i], 0, 1, axis=dim) for i in down])
    from_low = lax.ppermute(going_up, axis, [(i, (i + 1) % count) for i in range(count)])
    from_high = lax.ppermute(going_down, axis, [((i + 1) % count, i) for i in range(count)])
    fields = list(fields)
    for k, i in enumerate(up):
        kept = lax.slice_in_dim(fields[i], 0, extent - 1, axis=dim)
        fields[i] = jnp.concatenate([from_low[k], kept], axis=dim)
    for k, i in enumerate(down):
        kept = lax.slice_in_dim(fields[i], 1, extent, axis=dim)
        fields[i] = jnp.concatenate([kept, from_high[k]], axis=dim)
    return fields


def kernel_weights(offset):
    root_term = jnp.sqrt(1.0 + 4.0 * offset - 4.0 * offset * offset)
    return jnp.stack(
        [
            (3.0 - 2.0 * offset - root_term) / 8.0,
            (3.0 - 2.0 * offset + root_term) / 8.0,
            (1.0 + 2.0 * offset + root_term) / 8.0,
            (1.0 + 2.0 * offset - root_term) / 8.0,
        ]
    )


def collide(populations, forcing):
    density = jnp.sum(populations, axis=0)
    velocity = []
    for component in range(3):
        running = 0.5 * forcing[component]
        for direction in range(19):
            speed_value = lattice_speeds[direction][component]
            if speed_value != 0:
                running = running + speed_value * populations[direction]
        velocity.append(running / density)
    square = velocity[0] * velocity[0] + velocity[1] * velocity[1] + velocity[2] * velocity[2]
    collided = []
    for direction in range(19):
        speeds = lattice_speeds[direction]
        weight = lattice_weights[direction]
        contracted = jnp.zeros_like(density)
        for component in range(3):
            if speeds[component] != 0:
                contracted = contracted + speeds[component] * velocity[component]
        equilibrium = (
            weight
            * density
            * (1.0 + 3.0 * contracted + 4.5 * contracted * contracted - 1.5 * square)
        )
        source = jnp.zeros_like(density)
        for component in range(3):
            source = (
                source
                + (
                    3.0 * (speeds[component] - velocity[component])
                    + 9.0 * contracted * speeds[component]
                )
                * forcing[component]
            )
        present = populations[direction]
        collided.append(
            present
            - (present - equilibrium) / relaxation
            + (1.0 - 0.5 / relaxation) * weight * source
        )
    return (collided, jnp.stack(velocity))


def fold_ghost(ghost, sides, extents):
    for (axis, dim), extent in zip(sides, extents):
        count = lax.axis_size(axis)
        below = lax.slice_in_dim(ghost, 0, 1, axis=dim)
        above = lax.slice_in_dim(ghost, extent + 1, extent + 3, axis=dim)
        from_high = lax.ppermute(below, axis, [((i + 1) % count, i) for i in range(count)])
        from_low = lax.ppermute(above, axis, [(i, (i + 1) % count) for i in range(count)])
        low_pad = [(0, 0)] * ghost.ndim
        low_pad[dim] = (0, extent - 2)
        high_pad = [(0, 0)] * ghost.ndim
        high_pad[dim] = (extent - 1, 0)
        ghost = (
            lax.slice_in_dim(ghost, 1, extent + 1, axis=dim)
            + jnp.pad(from_low, low_pad)
            + jnp.pad(from_high, high_pad)
        )
    return ghost


def fold_rims(extended, which, extent):
    middle = lax.slice_in_dim(extended, 3, extent + 3, axis=which)
    low_rims = lax.slice_in_dim(extended, 0, 2, axis=which)
    high_rims = lax.slice_in_dim(extended, extent + 5, extent + 6, axis=which)
    low_pad = [(0, 0)] * extended.ndim
    low_pad[which] = (0, extent - 2)
    high_pad = [(0, 0)] * extended.ndim
    high_pad[which] = (extent - 1, 0)
    return middle + jnp.pad(low_rims, low_pad) + jnp.pad(high_rims, high_pad)


def band_matrix(coordinate, weight, extent, anchor):
    positions = lax.broadcasted_iota(jnp.int32, (coordinate.shape[0], extent), 1)
    running = jnp.zeros((coordinate.shape[0], extent), jnp.float32)
    for shift_step in range(4):
        running = running + jnp.where(
            positions == (coordinate + anchor + shift_step)[:, None],
            weight[shift_step][:, None],
            0.0,
        )
    return running


def spread_banded(forces, coordinates, weights, grid_sizes):
    band_first = band_matrix(coordinates[0], weights[0], grid_sizes[0], 0)
    band_second = band_matrix(coordinates[1], weights[1], grid_sizes[1], 0)
    band_third = band_matrix(coordinates[2], weights[2], grid_sizes[2], 0)
    partial_value = (
        forces[:, None, None, :]
        * band_first.T[None, :, None, :]
        * band_second.T[None, None, :, :]
    )
    partial_value = partial_value.reshape(-1, forces.shape[1])
    partial_value, band_third = lax.optimization_barrier((partial_value, band_third))
    product = jnp.dot(
        partial_value, band_third, precision=three_pass, preferred_element_type=jnp.float32
    )
    return product.reshape((3,) + grid_sizes)


def sample_banded(velocity_ext, coordinates, weights, grid_sizes):
    flat_velocity = velocity_ext.reshape(3 * grid_sizes[0] * grid_sizes[1], grid_sizes[2])
    band_first = band_matrix(coordinates[0], weights[0], grid_sizes[0], 1)
    band_second = band_matrix(coordinates[1], weights[1], grid_sizes[1], 1)
    band_third = band_matrix(coordinates[2], weights[2], grid_sizes[2], 1)
    contracted = jnp.dot(
        flat_velocity, band_third.T, precision=three_pass, preferred_element_type=jnp.float32
    )
    contracted = contracted.reshape(3, grid_sizes[0], grid_sizes[1], -1)
    return jnp.sum(
        contracted * band_first.T[None, :, None, :] * band_second.T[None, None, :, :],
        axis=(1, 2),
    )


def shards(populations, marker_force, marker_offset, marker_owner, marker_cell):
    count_first = lax.axis_size("gx")
    count_rest = lax.axis_size("gy") * lax.axis_size("gz")
    devices = count_first * count_rest
    capacity = max(4, 2 * MARK_DEV // devices)
    slot_count = devices * capacity
    owners = marker_owner[:, 0]
    row_order = lax.broadcasted_iota(jnp.int32, (MARK_DEV, MARK_DEV), 0)
    column_order = lax.broadcasted_iota(jnp.int32, (MARK_DEV, MARK_DEV), 1)
    earlier = (owners[:, None] == owners[None, :]) & (column_order < row_order)
    before = jnp.sum(earlier.astype(jnp.int32), axis=1)
    slot_index = owners * capacity + before
    placing = (
        slot_index[:, None] == lax.broadcasted_iota(jnp.int32, (MARK_DEV, slot_count), 1)
    ).astype(jnp.float32)
    record = jnp.concatenate(
        [marker_offset, marker_force, marker_cell.astype(jnp.float32)[None, :]], axis=0
    )
    buckets = jnp.dot(record, placing, precision=highest, preferred_element_type=jnp.float32)
    buckets = buckets.reshape(7, count_first, count_rest, capacity)
    received = lax.all_to_all(
        lax.all_to_all(buckets, "gx", split_axis=1, concat_axis=1, tiled=True),
        ("gy", "gz"),
        split_axis=2,
        concat_axis=2,
        tiled=True,
    )
    received = received.reshape(7, slot_count)
    forces = received[3:6]
    cell_index = received[6].astype(jnp.int32)
    coordinates = (cell_index // (CY * CZ), cell_index // CZ % CY, cell_index % CZ)
    weights = (
        kernel_weights(received[0]),
        kernel_weights(received[1]),
        kernel_weights(received[2]),
    )
    ghost_sizes = (CX + 3, CY + 3, CZ + 3)
    halo_sizes = (CX + 4, CY + 4, CZ + 4)
    ghost_field = spread_banded(forces, coordinates, weights, ghost_sizes)
    forcing = fold_ghost(ghost_field, (("gx", 1), ("gy", 2), ("gz", 3)), (CX, CY, CZ))
    collided, velocity = collide(populations, forcing)
    velocity_ext = extended_2(velocity, (("gx", 1), ("gy", 2), ("gz", 3)), 2)
    passed = collided
    for axis, dim in (("gx", 0), ("gy", 1), ("gz", 2)):
        passed = pass_axis(passed, axis, dim)
    new_populations = jnp.stack(passed)
    sampled = sample_banded(velocity_ext, coordinates, weights, halo_sizes)
    sampled = sampled.reshape(3, count_first, count_rest, capacity)
    returned = lax.all_to_all(
        lax.all_to_all(sampled, "gx", split_axis=1, concat_axis=1, tiled=True),
        ("gy", "gz"),
        split_axis=2,
        concat_axis=2,
        tiled=True,
    )
    returned = returned.reshape(3, slot_count)
    marker_velocity = jnp.dot(
        returned, placing.T, precision=highest, preferred_element_type=jnp.float32
    )
    return (new_populations, marker_velocity)


def solution(mesh):
    return jax.shard_map(
        shards,
        mesh=mesh,
        in_specs=(
            P(None, "gx", "gy", "gz"),
            P(None, ("gx", "gy", "gz")),
            P(None, ("gx", "gy", "gz")),
            P(("gx", "gy", "gz"), None),
            P(("gx", "gy", "gz")),
        ),
        out_specs=(P(None, "gx", "gy", "gz"), P(None, ("gx", "gy", "gz"))),
        check_vma=False,
    )
```

profile of v0, /device:TPU:1, one launch (start us, length us, event | category | flops | bytes accessed | tf_op | source)
XLA Modules:
  0.0 252.4 jit_solution(11942744003577986262)
XLA Ops:
  0.6 1.3 convert_reduce_fusion
  3.3 3.5 %fusion.1 = f32[7,2048]{1,0:T(8,128)S(1)} fusion(s32[1024]{0:T(1024)S(1)} %bitcast.785, f32[1,1024]{1,0:T(1,128)S(1)} %bitcast.788, f32[3,1024]{1,0:T(4,128)} %param.6, f32[3,1024]{1,0:T(4,128)} %param.7), kind=kOutput, calls=%fused_computation.3 | convolution fusion | flops 178272256 | bytes 90112 | tf_op jit(solution)/shard_map/dot_general | solution.py:221
  7.9 13.9 %all_to_all.20 = f32[16,1,896]{2,1,0:T(1,128)S(1)} all-to-all(f32[16,1,896]{2,1,0:T(1,128)S(1)} %reshape.855), channel_id=1, replica_groups=mesh['gx'=16,'gy'=4,'gz'=4] {'gx'}, dimensions={0} | all-to-all | bytes 114688 | tf_op jit(solution)/shard_map/all_to_all | solution.py:224
  23.7 18.3 %all_to_all.21 = f32[16,1,896]{2,1,0:T(1,128)S(1)} all-to-all(f32[16,1,896]{2,1,0:T(1,128)S(1)} %reshape.857), channel_id=1, replica_groups=mesh['gx'=16,'gy'=4,'gz'=4] {'gy','gz'}, dimensions={0} | all-to-all | bytes 114688 | tf_op jit(solution)/shard_map/all_to_all | solution.py:223
  45.0 5.7 %broadcast_multiply_fusion = f32[3,19,19,2048]{3,2,1,0:T(8,128)} fusion(f32[19,2048]{1,0:T(8,128)S(1)} %get-tuple-element.102, f32[3,19,2048]{2,1,0:T(8,128)S(1)} %broadcast_multiply_fusion.1), kind=kLoop, calls=%fused_computation.4 | loop fusion | flops 2217984 | bytes 9494528 | tf_op jit(solution)/shard_map/mul | solution.py:176
  50.7 10.4 %mul.1160 = f32[1083,2048]{1,0:T(8,128)} reshape(f32[3,19,19,2048]{3,2,1,0:T(8,128)} %broadcast_multiply_fusion) | data formatting | bytes 17743872 | tf_op jit(solution)/shard_map/mul | solution.py:176
  62.0 2.3 select_add_fusion
  64.3 9.8 %fusion.319 = f32[1083,259]{1,0:T(8,128)S(1)} fusion(f32[1083,2048]{1,0:T(8,128)} %mul.1160, f32[2048,259]{1,0:T(8,128)S(1)} %select_add_fusion), kind=kOutput, calls=%fused_computation.633 | convolution fusion | flops 3446747136 | bytes 12115652 | tf_op jit(solution)/shard_map/dot_general | solution.py:182
  74.1 1.5 reshape.841
  75.7 1.0 slice.626
  77.0 0.9 slice.627
  77.9 4.5 %collective-permute-start.1 = (f32[3,1,19,259]{3,2,1,0:T(8,128)S(1)}, f32[3,1,19,259]{3,2,1,0:T(8,128)S(1)}, u32[]{:S(2)}, u32[]{:S(2)}) collective-permute-start(f32[3,1,19,259]{3,2,1,0:T(8,128)S(1)} %slice.627), channel_id=1, source_target_pairs={{16,0},{32,16},{48,32},{64,48},{80,64},{96,80},{112,96},{128,112},... | collective-permute-start | bytes 177164 | tf_op jit(solution)/shard_map/ppermute | solution.py:134
  82.4 1.8 collective-permute-done.1
  84.1 2.5 collective-permute-done
  86.6 1.6 fusion.30
  88.3 1.6 collective-permute-start.2
  90.1 3.0 %reduce_sum.31 = f32[16,16,256]{2,1,0:T(8,128)S(1)} reduce(f32[19,16,16,256]{3,2,1,0:T(8,128)} %param.5, f32[]{:T(128)} %constant.146.clone.1), dimensions={0}, to_apply=%region_0.0 | reduce | flops 1179648 | bytes 5242884 | tf_op jit(solution)/shard_map/reduce_sum | solution.py:87
  93.1 6.7 %collective-permute-done.3 = f32[3,16,1,259]{3,2,1,0:T(1,128)S(1)} collective-permute-done((f32[3,16,1,259]{3,2,1,0:T(1,128)S(1)}, f32[3,16,1,259]{3,2,1,0:T(1,128)S(1)}, u32[]{:S(2)}, u32[]{:S(2)}) %collective-permute-start.3) | collective-permute-done | bytes 49760 | tf_op jit(solution)/shard_map/ppermute | solution.py:134
  100.2 1.3 collective-permute-start.4
  101.6 2.2 collective-permute-start.5
  103.8 0.9 select_add_fusion.1
  104.7 16.1 %collective-permute-done.5 = f32[3,16,16,1]{3,2,1,0:T(8,128)S(1)} collective-permute-done((f32[3,16,16,1]{3,2,1,0:T(8,128)S(1)}, f32[3,16,16,1]{3,2,1,0:T(8,128)S(1)}, u32[]{:S(2)}, u32[]{:S(2)}) %collective-permute-start.5) | collective-permute-done | bytes 3104 | tf_op jit(solution)/shard_map/ppermute | solution.py:134
  121.1 3.8 %fusion.279 = (f32[19,16,16,256]{3,2,1,0:T(8,128)}, f32[1,16,16,256]{3,2,1,0:T(8,128)S(1)}, f32[1,16,16,256]{3,2,1,0:T(8,128)S(1)}, f32[1,16,16,256]{3,2,1,0:T(8,128)S(1)}) fusion(f32[16,16,256]{2,1,0:T(8,128)S(1)} %reduce_sum.31, f32[19,16,16,256]{3,2,1,0:T(8,128)} %param.5, f32[3,16,16,256]{3,2,1,0:T(8,128)S(1)} %fusion.41), kind=kLoop, calls=%fused_computation.434 | loop fusion | flops 4784127 | bytes 7077888
  127.3 0.8 fusion.118
  128.1 0.8 fusion.132
  129.5 0.8 fusion.104
  130.5 0.8 slice.688
  131.5 4.8 %collective-permute-start.13 = (f32[3,2,16,256]{3,2,1,0:T(8,128)S(1)}, f32[3,2,16,256]{3,2,1,0:T(8,128)S(1)}, u32[]{:S(2)}, u32[]{:S(2)}) collective-permute-start(f32[3,2,16,256]{3,2,1,0:T(8,128)S(1)} %get-tuple-element.38), channel_id=1, source_target_pairs={{16,0},{32,16},{48,32},{64,48},{80,64},{96,80},{112,96},{128,112},... | collective-permute-start | bytes 294920 | tf_op jit(solution)/shard_map/ppermute | solution.py:48
  136.9 1.3 collective-permute-start.6
  139.8 3.7 %collective-permute-done.6 = f32[5,1,16,256]{3,2,1,0:T(8,128)S(1)} collective-permute-done((f32[5,1,16,256]{3,2,1,0:T(8,128)S(1)}, f32[5,1,16,256]{3,2,1,0:T(8,128)S(1)}, u32[]{:S(2)}, u32[]{:S(2)}) %collective-permute-start.6) | collective-permute-done | bytes 81952 | tf_op jit(solution)/shard_map/ppermute | solution.py:62
  143.6 3.4 %collective-permute-start.8 = (f32[5,16,1,256]{3,1,2,0:T(8,128)S(1)}, f32[5,16,1,256]{3,1,2,0:T(8,128)S(1)}, u32[]{:S(2)}, u32[]{:S(2)}) collective-permute-start(f32[5,16,1,256]{3,1,2,0:T(8,128)S(1)} %constant_dynamic-update-slice_fusion.10), channel_id=1, source_target_pairs={{0,4},{4,8},{8,12},{12,0},{1,5},{5,9},{9,13},{13,1},{2,6},{6,10},{... | collective-permute-start | bytes 245768 | tf_op jit(solution)/shard_map/ppermute | solution.py:62
  150.5 0.8 pad_maximum_fusion.17
  151.3 5.6 %collective-permute-start.14 = (f32[3,20,2,256]{3,2,1,0:T(2,128)}, f32[3,20,2,256]{3,2,1,0:T(2,128)}, u32[]{:S(2)}, u32[]{:S(2)}) collective-permute-start(f32[3,20,2,256]{3,2,1,0:T(2,128)} %get-tuple-element.35), channel_id=1, source_target_pairs={{0,4},{4,8},{8,12},{12,0},{1,5},{5,9},{9,13},{13,1},{2,6},{6,10},{... | collective-permute-start | bytes 368648 | tf_op jit(solution)/shard_map/ppermute | solution.py:46
  158.3 1.4 collective-permute-start.11
  164.8 0.8 copy.2983
  165.7 1.8 collective-permute-done.10
  167.4 1.4 slice_bitcast_fusion.33
  168.8 0.8 copy.2981
  169.6 0.8 copy.2986
  170.4 0.8 copy.2987
  171.3 0.9 copy.2988
  172.1 0.9 copy.2989
  173.0 1.9 fusion.187
  174.9 1.8 fusion.188
  176.7 1.7 fusion.182
  178.4 1.5 fusion.179
  179.9 1.7 fusion.176
  181.6 1.5 fusion.173
  183.0 1.8 fusion.170
  184.8 0.9 fusion.167
  185.7 0.9 fusion.164
  186.6 0.8 fusion.161
  187.8 1.6 fusion.158
  189.4 1.2 pad_maximum_fusion
  192.0 3.6 %collective-permute-start.17 = (f32[3,20,20,2]{2,3,1,0:T(2,128)S(1)}, f32[3,20,20,2]{2,3,1,0:T(2,128)S(1)}, u32[]{:S(2)}, u32[]{:S(2)}) collective-permute-start(f32[3,20,20,2]{2,3,1,0:T(2,128)S(1)} %copy.2995), channel_id=1, source_target_pairs={{1,0},{2,1},{3,2},{0,3},{5,4},{6,5},{7,6},{4,7},{9,8},{10,9},{11,1... | collective-permute-start | bytes 28808 | tf_op jit(solution)/shard_map/ppermute | solution.py:48
  195.5 0.9 fusion.155
  197.6 15.1 %multiply_reduce_fusion = f32[3,2048]{1,0:T(4,128)S(1)} fusion(f32[20,2048]{1,0:T(8,128)} %get-tuple-element.100, f32[20,2048]{1,0:T(8,128)} %get-tuple-element.101, f32[3,20,20,2]{3,2,1,0:T(8,128)S(1)} %copy.2997, f32[3,20,2,256]{3,2,1,0:T(2,128)} %collective-permute-done.15, f32[3,2,16,256]{3,2,1,0:T(8,128)S(1)} %copy-done.9, ...), kind=kOutput, calls=%fused_computation | convolution fusion | flops 3849575936 | bytes 1665792 | tf_op jit(solution)/shard_map/dot_general | solution.py:193
  213.9 3.5 %all-to-all-start.2 = ((f32[16,1,384]{2,1,0:T(1,128)}), f32[16,1,384]{2,1,0:T(1,128)S(1)}, u32[]{:S(2)}, u32[]{:S(2)}) async-start(f32[16,1,384]{2,1,0:T(1,128)} %reshape.859), calls=%async_computation.2 | async-start | bytes 49152 | tf_op jit(solution)/shard_map/all_to_all | solution.py:252
  217.4 0.9 fusion.152
  218.5 5.3 %all-to-all-done.2 = f32[16,1,384]{2,1,0:T(1,128)S(1)} async-done(((f32[16,1,384]{2,1,0:T(1,128)}), f32[16,1,384]{2,1,0:T(1,128)S(1)}, u32[]{:S(2)}, u32[]{:S(2)}) %all-to-all-start.2) | async-done | bytes 24608 | tf_op jit(solution)/shard_map/all_to_all | solution.py:252
  225.5 13.4 %all-to-all-start.3 = ((f32[16,1,384]{2,1,0:T(1,128)}), f32[16,1,384]{2,1,0:T(1,128)S(1)}, u32[]{:S(2)}, u32[]{:S(2)}) async-start(f32[16,1,384]{2,1,0:T(1,128)} %reshape.861), calls=%async_computation.3 | async-start | bytes 49152 | tf_op jit(solution)/shard_map/all_to_all | solution.py:251
  238.9 0.9 fusion.149
  239.8 6.5 %all-to-all-done.3 = f32[16,1,384]{2,1,0:T(1,128)S(1)} async-done(((f32[16,1,384]{2,1,0:T(1,128)}), f32[16,1,384]{2,1,0:T(1,128)S(1)}, u32[]{:S(2)}, u32[]{:S(2)}) %all-to-all-start.3) | async-done | bytes 24608 | tf_op jit(solution)/shard_map/all_to_all | solution.py:251
  247.5 4.5 %fusion = f32[3,1024]{1,0:T(4,128)} fusion(f32[3,2048]{1,0:T(4,128)S(1)} %reshape.843, s32[1024]{0:T(1024)S(1)} %bitcast.786), kind=kOutput, calls=%fused_computation.2 | convolution fusion | flops 77594624 | bytes 40960 | tf_op jit(solution)/shard_map/dot_general | solution.py:259
  (225 shorter events, 31.6 us)
Async XLA Ops:
  2.6 0.7 copy-start.31
  43.8 17.6 %copy-start.24 = (s32[2048]{0:T(1024)}, s32[2048]{0:T(1024)S(1)}, u32[]{:S(2)}) copy-start(s32[2048]{0:T(1024)S(1)} %get-tuple-element.74) | copy-start | bytes 24580
  43.8 17.6 %copy-start.25 = (s32[2048]{0:T(1024)}, s32[2048]{0:T(1024)S(1)}, u32[]{:S(2)}) copy-start(s32[2048]{0:T(1024)S(1)} %get-tuple-element.75) | copy-start | bytes 24580
  43.8 17.6 %copy-start.26 = (s32[2048]{0:T(1024)}, s32[2048]{0:T(1024)S(1)}, u32[]{:S(2)}) copy-start(s32[2048]{0:T(1024)S(1)} %get-tuple-element.76) | copy-start | bytes 24580
  61.3 0.6 copy-start.17
  61.4 0.6 copy-start.19
  61.4 0.6 copy-start.21
  61.4 0.6 copy-start.23
  76.6 10.0 %collective-permute-start = (f32[3,2,19,259]{3,2,1,0:T(8,128)S(1)}, f32[3,2,19,259]{3,2,1,0:T(8,128)S(1)}, u32[]{:S(2)}, u32[]{:S(2)}) collective-permute-start(f32[3,2,19,259]{3,2,1,0:T(8,128)S(1)} %slice.626), channel_id=1, source_target_pairs={{0,16},{16,32},{32,48},{48,64},{64,80},{80,96},{96,112},{112,128},... | collective-permute-start | bytes 354320 | tf_op jit(solution)/shard_map/ppermute | solution.py:135
  77.9 6.3 %collective-permute-start.1 = (f32[3,1,19,259]{3,2,1,0:T(8,128)S(1)}, f32[3,1,19,259]{3,2,1,0:T(8,128)S(1)}, u32[]{:S(2)}, u32[]{:S(2)}) collective-permute-start(f32[3,1,19,259]{3,2,1,0:T(8,128)S(1)} %slice.627), channel_id=1, source_target_pairs={{16,0},{32,16},{48,32},{64,48},{80,64},{96,80},{112,96},{128,112},... | collective-permute-start | bytes 177164 | tf_op jit(solution)/shard_map/ppermute | solution.py:134
  88.3 11.5 %collective-permute-start.2 = (f32[3,16,2,259]{3,2,1,0:T(2,128)S(1)}, f32[3,16,2,259]{3,2,1,0:T(2,128)S(1)}, u32[]{:S(2)}, u32[]{:S(2)}) collective-permute-start(f32[3,16,2,259]{3,2,1,0:T(2,128)S(1)} %slice.629), channel_id=1, source_target_pairs={{0,4},{4,8},{8,12},{12,0},{1,5},{5,9},{9,13},{13,1},{2,6},{6,10},{... | collective-permute-start | bytes 298376 | tf_op jit(solution)/shard_map/ppermute | solution.py:135
  90.0 9.9 %collective-permute-start.3 = (f32[3,16,1,259]{3,2,1,0:T(1,128)S(1)}, f32[3,16,1,259]{3,2,1,0:T(1,128)S(1)}, u32[]{:S(2)}, u32[]{:S(2)}) collective-permute-start(f32[3,16,1,259]{3,2,1,0:T(1,128)S(1)} %slice.630), channel_id=1, source_target_pairs={{4,0},{8,4},{12,8},{0,12},{5,1},{9,5},{13,9},{1,13},{6,2},{10,6},{... | collective-permute-start | bytes 149192 | tf_op jit(solution)/shard_map/ppermute | solution.py:134
  90.1 34.9 %slice-start = ((s8[4980736]{0:T(1024)(128)(4,1)}), s8[786432]{0:T(1024)(128)(4,1)S(1)}, s32[]{:S(2)}) async-start(s8[4980736]{0:T(1024)(128)(4,1)} %bitcast.767), calls=%async_computation.4 | async-start | bytes 1572864
  100.2 20.5 %collective-permute-start.4 = (f32[3,16,16,2]{3,2,1,0:T(8,128)S(1)}, f32[3,16,16,2]{3,2,1,0:T(8,128)S(1)}, u32[]{:S(2)}, u32[]{:S(2)}) collective-permute-start(f32[3,16,16,2]{3,2,1,0:T(8,128)S(1)} %slice.632), channel_id=1, source_target_pairs={{0,1},{1,2},{2,3},{3,0},{4,5},{5,6},{6,7},{7,4},{8,9},{9,10},{10,1... | collective-permute-start | bytes 18440 | tf_op jit(solution)/shard_map/ppermute | solution.py:135
  101.6 19.2 %collective-permute-start.5 = (f32[3,16,16,1]{3,2,1,0:T(8,128)S(1)}, f32[3,16,16,1]{3,2,1,0:T(8,128)S(1)}, u32[]{:S(2)}, u32[]{:S(2)}) collective-permute-start(f32[3,16,16,1]{3,2,1,0:T(8,128)S(1)} %slice.633), channel_id=1, source_target_pairs={{1,0},{2,1},{3,2},{0,3},{5,4},{6,5},{7,6},{4,7},{9,8},{10,9},{11,1... | collective-permute-start | bytes 9224 | tf_op jit(solution)/shard_map/ppermute | solution.py:134
  103.8 21.2 %slice-start.1 = ((s8[4980736]{0:T(1024)(128)(4,1)}), s8[4194304]{0:T(1024)(128)(4,1)S(1)}, s32[]{:S(2)}) async-start(s8[4980736]{0:T(1024)(128)(4,1)} %bitcast.767), calls=%async_computation.5 | async-start | bytes 8388608
  127.3 10.9 %copy-start.3 = (f32[16,16,256]{2,1,0:T(8,128)}, f32[16,16,256]{2,1,0:T(8,128)S(1)}, u32[]{:S(2)}) copy-start(f32[16,16,256]{2,1,0:T(8,128)S(1)} %get-tuple-element.16) | copy-start | bytes 786436
  131.4 19.1 %collective-permute-start.12 = (f32[3,2,16,256]{3,2,1,0:T(8,128)S(1)}, f32[3,2,16,256]{3,2,1,0:T(8,128)S(1)}, u32[]{:S(2)}, u32[]{:S(2)}) collective-permute-start(f32[3,2,16,256]{3,2,1,0:T(8,128)S(1)} %get-tuple-element.37), channel_id=1, source_target_pairs={{0,16},{16,32},{32,48},{48,64},{64,80},{80,96},{96,112},{112,128},... | collective-permute-start | bytes 294920 | tf_op jit(solution)/shard_map/ppermute | solution.py:46
  131.5 19.0 %collective-permute-start.13 = (f32[3,2,16,256]{3,2,1,0:T(8,128)S(1)}, f32[3,2,16,256]{3,2,1,0:T(8,128)S(1)}, u32[]{:S(2)}, u32[]{:S(2)}) collective-permute-start(f32[3,2,16,256]{3,2,1,0:T(8,128)S(1)} %get-tuple-element.38), channel_id=1, source_target_pairs={{16,0},{32,16},{48,32},{64,48},{80,64},{96,80},{112,96},{128,112},... | collective-permute-start | bytes 294920 | tf_op jit(solution)/shard_map/ppermute | solution.py:48
  136.4 3.4 %collective-permute-start.7 = (f32[5,1,16,256]{3,2,1,0:T(8,128)S(1)}, f32[5,1,16,256]{3,2,1,0:T(8,128)S(1)}, u32[]{:S(2)}, u32[]{:S(2)}) collective-permute-start(f32[5,1,16,256]{3,2,1,0:T(8,128)S(1)} %constant_dynamic-update-slice_fusion.5), channel_id=1, source_target_pairs={{16,0},{32,16},{48,32},{64,48},{80,64},{96,80},{112,96},{128,112},... | collective-permute-start | bytes 245768 | tf_op jit(solution)/shard_map/ppermute | solution.py:63
  136.7 13.7 %copy-start.2 = (f32[15,16,256]{2,1,0:T(8,128)}, f32[15,16,256]{2,1,0:T(8,128)S(1)}, u32[]{:S(2)}) copy-start(f32[15,16,256]{2,1,0:T(8,128)S(1)} %slice.653) | copy-start | bytes 737284
  136.7 11.1 %copy-start.1 = (f32[15,16,256]{2,1,0:T(8,128)}, f32[15,16,256]{2,1,0:T(8,128)S(1)}, u32[]{:S(2)}) copy-start(f32[15,16,256]{2,1,0:T(8,128)S(1)} %slice.665) | copy-start | bytes 737284
  136.8 10.8 %copy-start = (f32[15,16,256]{2,1,0:T(8,128)}, f32[15,16,256]{2,1,0:T(8,128)S(1)}, u32[]{:S(2)}) copy-start(f32[15,16,256]{2,1,0:T(8,128)S(1)} %slice.671) | copy-start | bytes 737284
  136.9 6.7 %collective-permute-start.6 = (f32[5,1,16,256]{3,2,1,0:T(8,128)S(1)}, f32[5,1,16,256]{3,2,1,0:T(8,128)S(1)}, u32[]{:S(2)}, u32[]{:S(2)}) collective-permute-start(f32[5,1,16,256]{3,2,1,0:T(8,128)S(1)} %constant_dynamic-update-slice_fusion), channel_id=1, source_target_pairs={{0,16},{16,32},{32,48},{48,64},{64,80},{80,96},{96,112},{112,128},... | collective-permute-start | bytes 245768 | tf_op jit(solution)/shard_map/ppermute | solution.py:62
  143.6 13.3 %collective-permute-start.8 = (f32[5,16,1,256]{3,1,2,0:T(8,128)S(1)}, f32[5,16,1,256]{3,1,2,0:T(8,128)S(1)}, u32[]{:S(2)}, u32[]{:S(2)}) collective-permute-start(f32[5,16,1,256]{3,1,2,0:T(8,128)S(1)} %constant_dynamic-update-slice_fusion.10), channel_id=1, source_target_pairs={{0,4},{4,8},{8,12},{12,0},{1,5},{5,9},{9,13},{13,1},{2,6},{6,10},{... | collective-permute-start | bytes 245768 | tf_op jit(solution)/shard_map/ppermute | solution.py:62
  147.1 10.5 %collective-permute-start.9 = (f32[5,16,1,256]{3,2,1,0:T(1,128)S(1)}, f32[5,16,1,256]{3,2,1,0:T(1,128)S(1)}, u32[]{:S(2)}, u32[]{:S(2)}) collective-permute-start(f32[5,16,1,256]{3,2,1,0:T(1,128)S(1)} %constant_dynamic-update-slice_fusion.15), channel_id=1, source_target_pairs={{4,0},{8,4},{12,8},{0,12},{5,1},{9,5},{13,9},{1,13},{6,2},{10,6},{... | collective-permute-start | bytes 245768 | tf_op jit(solution)/shard_map/ppermute | solution.py:63
  150.4 38.9 %copy-start.6 = (f32[3,2,16,256]{3,2,1,0:T(8,128)}, f32[3,2,16,256]{3,2,1,0:T(8,128)S(1)}, u32[]{:S(2)}) copy-start(f32[3,2,16,256]{3,2,1,0:T(8,128)S(1)} %collective-permute-done.12) | copy-start | bytes 294916
  150.4 21.7 %copy-start.8 = (f32[3,2,16,256]{3,2,1,0:T(8,128)}, f32[3,2,16,256]{3,2,1,0:T(8,128)S(1)}, u32[]{:S(2)}) copy-start(f32[3,2,16,256]{3,2,1,0:T(8,128)S(1)} %collective-permute-done.13) | copy-start | bytes 294916
  151.3 38.1 %collective-permute-start.14 = (f32[3,20,2,256]{3,2,1,0:T(2,128)}, f32[3,20,2,256]{3,2,1,0:T(2,128)}, u32[]{:S(2)}, u32[]{:S(2)}) collective-permute-start(f32[3,20,2,256]{3,2,1,0:T(2,128)} %get-tuple-element.35), channel_id=1, source_target_pairs={{0,4},{4,8},{8,12},{12,0},{1,5},{5,9},{9,13},{13,1},{2,6},{6,10},{... | collective-permute-start | bytes 368648 | tf_op jit(solution)/shard_map/ppermute | solution.py:46
  156.9 32.5 %collective-permute-start.15 = (f32[3,20,2,256]{3,2,1,0:T(2,128)}, f32[3,20,2,256]{3,2,1,0:T(2,128)}, u32[]{:S(2)}, u32[]{:S(2)}) collective-permute-start(f32[3,20,2,256]{3,2,1,0:T(2,128)} %get-tuple-element.36), channel_id=1, source_target_pairs={{4,0},{8,4},{12,8},{0,12},{5,1},{9,5},{13,9},{1,13},{6,2},{10,6},{... | collective-permute-start | bytes 368648 | tf_op jit(solution)/shard_map/ppermute | solution.py:48
  156.9 0.6 copy-start.14
  158.2 14.0 %copy-start.10 = (f32[16,1,256]{2,1,0:T(1,128)}, f32[16,1,256]{2,1,0:T(1,128)S(1)}, u32[]{:S(2)}) copy-start(f32[16,1,256]{2,1,0:T(1,128)S(1)} %get-tuple-element.51) | copy-start | bytes 49156
  158.2 14.0 %copy-start.12 = (f32[16,1,256]{2,1,0:T(1,128)}, f32[16,1,256]{2,1,0:T(1,128)S(1)}, u32[]{:S(2)}) copy-start(f32[16,1,256]{2,1,0:T(1,128)S(1)} %get-tuple-element.50) | copy-start | bytes 49156
  158.3 5.9 %collective-permute-start.11 = (f32[5,16,16,1]{2,1,3,0:T(8,128)S(1)}, f32[5,16,16,1]{2,1,3,0:T(8,128)S(1)}, u32[]{:S(2)}, u32[]{:S(2)}) collective-permute-start(f32[5,16,16,1]{2,1,3,0:T(8,128)S(1)} %constant_dynamic-update-slice_fusion.25), channel_id=1, source_target_pairs={{1,0},{2,1},{3,2},{0,3},{5,4},{6,5},{7,6},{4,7},{9,8},{10,9},{11,1... | collective-permute-start | bytes 15368 | tf_op jit(solution)/shard_map/ppermute | solution.py:63
  159.7 11.6 %copy-start.16 = (f32[16,1,256]{2,1,0:T(1,128)}, f32[16,1,256]{2,1,0:T(1,128)S(1)}, u32[]{:S(2)}) copy-start(f32[16,1,256]{2,1,0:T(1,128)S(1)} %copy.2980) | copy-start | bytes 49156
  161.3 6.1 %collective-permute-start.10 = (f32[5,16,16,1]{2,1,3,0:T(8,128)}, f32[5,16,16,1]{2,1,3,0:T(8,128)}, u32[]{:S(2)}, u32[]{:S(2)}) collective-permute-start(f32[5,16,16,1]{2,1,3,0:T(8,128)} %constant_dynamic-update-slice_fusion.20), channel_id=1, source_target_pairs={{0,1},{1,2},{2,3},{3,0},{4,5},{5,6},{6,7},{7,4},{8,9},{9,10},{10,1... | collective-permute-start | bytes 15368 | tf_op jit(solution)/shard_map/ppermute | solution.py:62
  173.0 10.0 %copy-start.5 = (f32[16,16,1]{2,1,0:T(8,128)S(1)}, f32[16,16,1]{2,1,0:T(8,128)}, u32[]{:S(2)}) copy-start(f32[16,16,1]{2,1,0:T(8,128)} %copy.2986) | copy-start | bytes 3076
  173.0 11.8 %copy-start.4 = (f32[16,16,1]{2,1,0:T(8,128)S(1)}, f32[16,16,1]{2,1,0:T(8,128)}, u32[]{:S(2)}) copy-start(f32[16,16,1]{2,1,0:T(8,128)} %copy.2987) | copy-start | bytes 3076
  178.4 9.0 %copy-start.30 = (f32[16,16,1]{1,0,2:T(8,128)S(1)}, f32[16,16,1]{1,0,2:T(8,128)}, u32[]{:S(2)}) copy-start(f32[16,16,1]{1,0,2:T(8,128)} %get-tuple-element.64) | copy-start | bytes 3076
  178.4 9.2 %copy-start.29 = (f32[16,16,1]{1,0,2:T(8,128)S(1)}, f32[16,16,1]{1,0,2:T(8,128)}, u32[]{:S(2)}) copy-start(f32[16,16,1]{1,0,2:T(8,128)} %get-tuple-element.69) | copy-start | bytes 3076
  189.3 6.2 %copy-start.13 = (f32[16,1,256]{2,1,0:T(1,128)S(1)}, f32[16,1,256]{2,1,0:T(1,128)}, u32[]{:S(2)}) copy-start(f32[16,1,256]{2,1,0:T(1,128)} %copy-done.12) | copy-start | bytes 49156
  190.6 5.8 %copy-start.28 = (f32[16,16,1]{1,0,2:T(8,128)S(1)}, f32[16,16,1]{1,0,2:T(8,128)}, u32[]{:S(2)}) copy-start(f32[16,16,1]{1,0,2:T(8,128)} %get-tuple-element.68) | copy-start | bytes 3076
  190.6 7.0 %copy-start.7 = (f32[3,2,16,256]{3,2,1,0:T(8,128)S(1)}, f32[3,2,16,256]{3,2,1,0:T(8,128)}, u32[]{:S(2)}) copy-start(f32[3,2,16,256]{3,2,1,0:T(8,128)} %copy-done.6) | copy-start | bytes 294916
  190.6 6.9 %copy-start.9 = (f32[3,2,16,256]{3,2,1,0:T(8,128)S(1)}, f32[3,2,16,256]{3,2,1,0:T(8,128)}, u32[]{:S(2)}) copy-start(f32[3,2,16,256]{3,2,1,0:T(8,128)} %copy-done.8) | copy-start | bytes 294916
  190.6 6.9 %copy-start.18 = (f32[2048]{0:T(1024)S(1)}, f32[2048]{0:T(1024)}, u32[]{:S(2)}) copy-start(f32[2048]{0:T(1024)} %copy-done.17) | copy-start | bytes 24580
  190.7 6.9 %copy-start.20 = (f32[2048]{0:T(1024)S(1)}, f32[2048]{0:T(1024)}, u32[]{:S(2)}) copy-start(f32[2048]{0:T(1024)} %copy-done.19) | copy-start | bytes 24580
  190.7 6.9 %copy-start.22 = (f32[2048]{0:T(1024)S(1)}, f32[2048]{0:T(1024)}, u32[]{:S(2)}) copy-start(f32[2048]{0:T(1024)} %copy-done.21) | copy-start | bytes 24580
  191.4 5.2 %collective-permute-start.16 = (f32[3,20,20,2]{2,3,1,0:T(2,128)S(1)}, f32[3,20,20,2]{2,3,1,0:T(2,128)S(1)}, u32[]{:S(2)}, u32[]{:S(2)}) collective-permute-start(f32[3,20,20,2]{2,3,1,0:T(2,128)S(1)} %copy.2994), channel_id=1, source_target_pairs={{0,1},{1,2},{2,3},{3,0},{4,5},{5,6},{6,7},{7,4},{8,9},{9,10},{10,1... | collective-permute-start | bytes 28808 | tf_op jit(solution)/shard_map/ppermute | solution.py:46
  192.0 5.1 %collective-permute-start.17 = (f32[3,20,20,2]{2,3,1,0:T(2,128)S(1)}, f32[3,20,20,2]{2,3,1,0:T(2,128)S(1)}, u32[]{:S(2)}, u32[]{:S(2)}) collective-permute-start(f32[3,20,20,2]{2,3,1,0:T(2,128)S(1)} %copy.2995), channel_id=1, source_target_pairs={{1,0},{2,1},{3,2},{0,3},{5,4},{6,5},{7,6},{4,7},{9,8},{10,9},{11,1... | collective-permute-start | bytes 28808 | tf_op jit(solution)/shard_map/ppermute | solution.py:48
  197.6 19.8 %copy-start.15 = (f32[16,1,256]{2,1,0:T(1,128)S(1)}, f32[16,1,256]{2,1,0:T(1,128)}, u32[]{:S(2)}) copy-start(f32[16,1,256]{2,1,0:T(1,128)} %copy-done.14) | copy-start | bytes 49156
  197.6 20.7 %copy-start.27 = (f32[16,16,1]{1,0,2:T(8,128)S(1)}, f32[16,16,1]{1,0,2:T(8,128)}, u32[]{:S(2)}) copy-start(f32[16,16,1]{1,0,2:T(8,128)} %get-tuple-element.63) | copy-start | bytes 3076
  197.6 41.3 %copy-start.11 = (f32[16,1,256]{2,1,0:T(1,128)S(1)}, f32[16,1,256]{2,1,0:T(1,128)}, u32[]{:S(2)}) copy-start(f32[16,1,256]{2,1,0:T(1,128)} %copy-done.10) | copy-start | bytes 49156
  212.8 34.7 %copy-start.32 = (s32[1024,1]{0,1:T(1,128)S(1)}, s32[1024,1]{0,1:T(1,128)}, u32[]{:S(2)}) copy-start(s32[1024,1]{0,1:T(1,128)} %copy-done.31) | copy-start | bytes 12292
  213.9 9.9 %all-to-all-start.2 = ((f32[16,1,384]{2,1,0:T(1,128)}), f32[16,1,384]{2,1,0:T(1,128)S(1)}, u32[]{:S(2)}, u32[]{:S(2)}) async-start(f32[16,1,384]{2,1,0:T(1,128)} %reshape.859), calls=%async_computation.2 | async-start | bytes 49152 | tf_op jit(solution)/shard_map/all_to_all | solution.py:252
  225.5 20.7 %all-to-all-start.3 = ((f32[16,1,384]{2,1,0:T(1,128)}), f32[16,1,384]{2,1,0:T(1,128)S(1)}, u32[]{:S(2)}, u32[]{:S(2)}) async-start(f32[16,1,384]{2,1,0:T(1,128)} %reshape.861), calls=%async_computation.3 | async-start | bytes 49152 | tf_op jit(solution)/shard_map/all_to_all | solution.py:251
where the time goes:
time: 257 us; the launch traced here: 252 us
  other arithmetic  54.6 us (21%)
  starting transfers between devices  47.7 us (19%)
  waiting for transfers between devices  45 us (18%)
  local copies, waits for them, and re-layouts  37.9 us (15%)
  matrix products  32.9 us (13%)
  blocking collectives  32.2 us (13%)
    unnamed x21, other arithmetic  24.6 us
    ppermute x3, waiting for transfers between devices, fold_ghost(): lax.ppermute(below, axis, [((i + 1) % count, i) for i in range(count)])  24.6 us
    all_to_all x1, blocking collectives, shards(): lax.all_to_all(lax.all_to_all(buckets, 'gx', split_axis=1, concat_axis=1,...  18.3 us
    dot_general x1, matrix products, sample_banded(): jnp.dot(flat_velocity, band_third.T, precision=three_pass, preferred_elem...  15.1 us
    all_to_all x1, blocking collectives, shards(): lax.all_to_all(buckets, 'gx', split_axis=1, concat_axis=1, tiled=True)  13.9 us
    all_to_all x1, starting transfers between devices, shards(): lax.all_to_all(lax.all_to_all(sampled, 'gx', split_axis=1, concat_axis=1,...  13.4 us
    mul x2, local copies, waits for them, and re-layouts, spread_banded(): forces[:, None, None, :] * band_first.T[None, :, None, :]  10.6 us
    dot_general x1, matrix products, spread_banded(): jnp.dot(partial_value, band_third, precision=three_pass, preferred_elemen...  9.81 us
  transfers between devices with their start and end apart: 20, of which 9 were waited for; matrix products, arithmetic and copies ran while one was open for 17% of the time, Pallas kernels for 0%

commit v1 on v0

--- a/solution.py
+++ b/solution.py
@@ -36,6 +36,22 @@
 three_pass = lax.Precision.HIGH
 
 
+def extended(cells, sides, low, high):
+    for axis, dim in sides:
+        count = lax.axis_size(axis)
+        head = lax.slice_in_dim(cells, 0, high, axis=dim)
+        tail = lax.slice_in_dim(cells, cells.shape[dim] - low, cells.shape[dim], axis=dim)
+        cells = jnp.concatenate(
+            [
+                lax.ppermute(tail, axis, [(i, (i + 1) % count) for i in range(count)]),
+                cells,
+                lax.ppermute(head, axis, [((i + 1) % count, i) for i in range(count)]),
+            ],
+            axis=dim,
+        )
+    return cells
+
+
 def extended_2(cells, sides, width):
     for axis, dim in sides:
         count = lax.axis_size(axis)
@@ -185,11 +201,11 @@
     return product.reshape((3,) + grid_sizes)
 
 
-def sample_banded(velocity_ext, coordinates, weights, grid_sizes):
+def sample_banded(velocity_ext, coordinates, weights, grid_sizes, anchor):
     flat_velocity = velocity_ext.reshape(3 * grid_sizes[0] * grid_sizes[1], grid_sizes[2])
-    band_first = band_matrix(coordinates[0], weights[0], grid_sizes[0], 1)
-    band_second = band_matrix(coordinates[1], weights[1], grid_sizes[1], 1)
-    band_third = band_matrix(coordinates[2], weights[2], grid_sizes[2], 1)
+    band_first = band_matrix(coordinates[0], weights[0], grid_sizes[0], anchor)
+    band_second = band_matrix(coordinates[1], weights[1], grid_sizes[1], anchor)
+    band_third = band_matrix(coordinates[2], weights[2], grid_sizes[2], anchor)
     contracted = jnp.dot(
         flat_velocity, band_third.T, precision=three_pass, preferred_element_type=jnp.float32
     )
@@ -237,16 +253,15 @@
         kernel_weights(received[2]),
     )
     ghost_sizes = (CX + 3, CY + 3, CZ + 3)
-    halo_sizes = (CX + 4, CY + 4, CZ + 4)
     ghost_field = spread_banded(forces, coordinates, weights, ghost_sizes)
     forcing = fold_ghost(ghost_field, (("gx", 1), ("gy", 2), ("gz", 3)), (CX, CY, CZ))
     collided, velocity = collide(populations, forcing)
-    velocity_ext = extended_2(velocity, (("gx", 1), ("gy", 2), ("gz", 3)), 2)
+    velocity_ext = extended(velocity, (("gx", 1), ("gy", 2), ("gz", 3)), 1, 2)
     passed = collided
     for axis, dim in (("gx", 0), ("gy", 1), ("gz", 2)):
         passed = pass_axis(passed, axis, dim)
     new_populations = jnp.stack(passed)
-    sampled = sample_banded(velocity_ext, coordinates, weights, halo_sizes)
+    sampled = sample_banded(velocity_ext, coordinates, weights, ghost_sizes, 0)
     sampled = sampled.reshape(3, count_first, count_rest, capacity)
     returned = lax.all_to_all(
         lax.all_to_all(sampled, "gx", split_axis=1, concat_axis=1, tiled=True),

time: 257 us -> 264 us (1.027)
  local copies, waits for them, and re-layouts: 37.9 us -> 46 us
  waiting for transfers between devices: 45 us -> 48.5 us
  other arithmetic: 54.6 us -> 51.4 us
    ppermute x3, starting transfers between devices: 1.75 us -> 5.93 us  [pass_axis(): lax.ppermute(going_down, axis, [((i + 1) % count, i) for i in range(count)])]
    ppermute x6, starting transfers between devices: 14.1 us -> 10.7 us  [the longest x3 5.95 us: extended(): lax.ppermute(tail, axis, [(i, (i + 1) % count) for i in range(count)])]
    squeeze x8, local copies, waits for them, and re-layouts: 4.07 us -> 7.45 us  [pass_axis(): fields[i] = jnp.concatenate([kept, from_high[k]], axis=dim)]
    squeeze x13, local copies, waits for them, and re-layouts: 5.5 us -> 8.88 us  [pass_axis(): fields[i] = jnp.concatenate([from_low[k], kept], axis=dim)]
    unnamed x100 -> x108, local copies, waits for them, and re-layouts: 6.11 us -> 6.17 us
  transfers between devices with their start and end apart: 20 -> 20, of which waited for: 9 -> 10; matrix products, arithmetic and copies ran while one was open for 17% -> 19% of each run, Pallas kernels for 0% -> 0%
where the time goes in v1:
time: 264 us; the launch traced here: 259 us
  other arithmetic  51.4 us (19%)
  waiting for transfers between devices  48.5 us (18%)
  starting transfers between devices  46.8 us (18%)
  local copies, waits for them, and re-layouts  46 us (17%)
  blocking collectives  32.2 us (12%)
  matrix products  31.4 us (12%)
    ppermute x3, waiting for transfers between devices, fold_ghost(): lax.ppermute(below, axis, [((i + 1) % count, i) for i in range(count)])  25.6 us
    unnamed x21, other arithmetic  24.3 us
    all_to_all x1, blocking collectives, shards(): lax.all_to_all(lax.all_to_all(buckets, 'gx', split_axis=1, concat_axis=1,...  18.3 us
    all_to_all x1, blocking collectives, shards(): lax.all_to_all(buckets, 'gx', split_axis=1, concat_axis=1, tiled=True)  13.9 us
    dot_general x1, matrix products, sample_banded(): jnp.dot(flat_velocity, band_third.T, precision=three_pass, preferred_elem...  13.8 us
    all_to_all x1, starting transfers between devices, shards(): lax.all_to_all(lax.all_to_all(sampled, 'gx', split_axis=1, concat_axis=1,...  12.1 us
    mul x2, local copies, waits for them, and re-layouts, spread_banded(): forces[:, None, None, :] * band_first.T[None, :, None, :]  10.6 us
    dot_general x1, matrix products, spread_banded(): jnp.dot(partial_value, band_third, precision=three_pass, preferred_elemen...  9.72 us
  transfers between devices with their start and end apart: 20, of which 10 were waited for; matrix products, arithmetic and copies ran while one was open for 19% of the time, Pallas kernels for 0%

profile of v1, /device:TPU:1, one launch (start us, length us, event | category | flops | bytes accessed | tf_op | source)
XLA Modules:
  0.0 258.6 jit_solution(5090788743195469930)
XLA Ops:
  0.6 1.3 convert_reduce_fusion
  3.3 3.5 %fusion.1 = f32[7,2048]{1,0:T(8,128)S(1)} fusion(s32[1024]{0:T(1024)S(1)} %bitcast.785, f32[1,1024]{1,0:T(1,128)S(1)} %bitcast.788, f32[3,1024]{1,0:T(4,128)} %param.6, f32[3,1024]{1,0:T(4,128)} %param.7), kind=kOutput, calls=%fused_computation.3 | convolution fusion | flops 178272256 | bytes 90112 | tf_op jit(solution)/shard_map/dot_general | solution.py:237
  7.9 13.9 %all_to_all.20 = f32[16,1,896]{2,1,0:T(1,128)S(1)} all-to-all(f32[16,1,896]{2,1,0:T(1,128)S(1)} %reshape.508), channel_id=1, replica_groups=mesh['gx'=16,'gy'=4,'gz'=4] {'gx'}, dimensions={0} | all-to-all | bytes 114688 | tf_op jit(solution)/shard_map/all_to_all | solution.py:240
  23.5 18.3 %all_to_all.21 = f32[16,1,896]{2,1,0:T(1,128)S(1)} all-to-all(f32[16,1,896]{2,1,0:T(1,128)S(1)} %reshape.510), channel_id=1, replica_groups=mesh['gx'=16,'gy'=4,'gz'=4] {'gy','gz'}, dimensions={0} | all-to-all | bytes 114688 | tf_op jit(solution)/shard_map/all_to_all | solution.py:239
  44.9 5.7 %broadcast_multiply_fusion = f32[3,19,19,2048]{3,2,1,0:T(8,128)} fusion(f32[19,2048]{1,0:T(8,128)S(1)} %get-tuple-element.91, f32[3,19,2048]{2,1,0:T(8,128)S(1)} %broadcast_multiply_fusion.1), kind=kLoop, calls=%fused_computation.4 | loop fusion | flops 2217984 | bytes 9494528 | tf_op jit(solution)/shard_map/mul | solution.py:192
  50.6 10.4 %mul.1158 = f32[1083,2048]{1,0:T(8,128)} reshape(f32[3,19,19,2048]{3,2,1,0:T(8,128)} %broadcast_multiply_fusion) | data formatting | bytes 17743872 | tf_op jit(solution)/shard_map/mul | solution.py:192
  62.1 9.7 %fusion.301 = f32[1083,259]{1,0:T(8,128)S(1)} fusion(f32[1083,2048]{1,0:T(8,128)} %mul.1158, f32[2048,259]{0,1:T(8,128)S(1)} %select_add_fusion), kind=kOutput, calls=%fused_computation.598 | convolution fusion | flops 3446747136 | bytes 12115652 | tf_op jit(solution)/shard_map/dot_general | solution.py:198
  71.9 1.5 reshape.494
  73.4 1.0 slice.626
  74.7 0.9 slice.627
  75.6 4.5 %collective-permute-start.1 = (f32[3,1,19,259]{3,2,1,0:T(8,128)S(1)}, f32[3,1,19,259]{3,2,1,0:T(8,128)S(1)}, u32[]{:S(2)}, u32[]{:S(2)}) collective-permute-start(f32[3,1,19,259]{3,2,1,0:T(8,128)S(1)} %slice.627), channel_id=1, source_target_pairs={{16,0},{32,16},{48,32},{64,48},{80,64},{96,80},{112,96},{128,112},... | collective-permute-start | bytes 177164 | tf_op jit(solution)/shard_map/ppermute | solution.py:150
  80.1 1.8 collective-permute-done.1
  81.9 2.5 collective-permute-done
  84.4 1.6 fusion.23
  86.1 1.6 collective-permute-start.2
  87.8 9.8 %collective-permute-done.3 = f32[3,16,1,259]{3,2,1,0:T(1,128)S(1)} collective-permute-done((f32[3,16,1,259]{3,2,1,0:T(1,128)S(1)}, f32[3,16,1,259]{3,2,1,0:T(1,128)S(1)}, u32[]{:S(2)}, u32[]{:S(2)}) %collective-permute-start.3) | collective-permute-done | bytes 49760 | tf_op jit(solution)/shard_map/ppermute | solution.py:150
  98.0 1.2 collective-permute-start.4
  99.2 2.4 collective-permute-start.5
  101.6 2.9 %reduce_sum.31 = f32[16,16,256]{2,1,0:T(8,128)S(1)} reduce(f32[19,16,16,256]{3,2,1,0:T(8,128)} %param.5, f32[]{:T(128)} %constant.137.clone.1), dimensions={0}, to_apply=%region_0.0 | reduce | flops 1179648 | bytes 5242884 | tf_op jit(solution)/shard_map/reduce_sum | solution.py:103
  104.6 14.0 %collective-permute-done.5 = f32[3,16,16,1]{3,2,1,0:T(8,128)S(1)} collective-permute-done((f32[3,16,16,1]{3,2,1,0:T(8,128)S(1)}, f32[3,16,16,1]{3,2,1,0:T(8,128)S(1)}, u32[]{:S(2)}, u32[]{:S(2)}) %collective-permute-start.5) | collective-permute-done | bytes 3104 | tf_op jit(solution)/shard_map/ppermute | solution.py:150
  119.0 4.0 %fusion.263 = (f32[19,16,16,256]{3,2,1,0:T(8,128)}, f32[1,16,16,256]{3,2,1,0:T(8,128)S(1)}, f32[1,16,16,256]{3,2,1,0:T(8,128)S(1)}, f32[1,16,16,256]{3,2,1,0:T(8,128)S(1)}) fusion(f32[16,16,256]{2,1,0:T(8,128)S(1)} %reduce_sum.31, f32[19,16,16,256]{3,2,1,0:T(8,128)} %param.5, f32[3,16,16,256]{3,2,1,0:T(8,128)S(1)} %fusion.25), kind=kLoop, calls=%fused_computation.414 | loop fusion | flops 4784127 | bytes 7077888
  125.4 0.8 fusion.102
  128.6 0.8 slice.688
  129.5 3.2 %collective-permute-start.13 = (f32[3,2,16,256]{3,2,1,0:T(8,128)S(1)}, f32[3,2,16,256]{3,2,1,0:T(8,128)S(1)}, u32[]{:S(2)}, u32[]{:S(2)}) collective-permute-start(f32[3,2,16,256]{3,2,1,0:T(8,128)S(1)} %pad_maximum_fusion.17), channel_id=1, source_target_pairs={{16,0},{32,16},{48,32},{64,48},{80,64},{96,80},{112,96},{128,112},... | collective-permute-start | bytes 294920 | tf_op jit(solution)/shard_map/ppermute | solution.py:48
  132.9 4.9 %collective-permute-start.7 = (f32[5,1,16,256]{3,2,1,0:T(8,128)S(1)}, f32[5,1,16,256]{3,2,1,0:T(8,128)S(1)}, u32[]{:S(2)}, u32[]{:S(2)}) collective-permute-start(f32[5,1,16,256]{3,2,1,0:T(8,128)S(1)} %constant_dynamic-update-slice_fusion.5), channel_id=1, source_target_pairs={{16,0},{32,16},{48,32},{64,48},{80,64},{96,80},{112,96},{128,112},... | collective-permute-start | bytes 245768 | tf_op jit(solution)/shard_map/ppermute | solution.py:79
  139.3 5.3 %collective-permute-done.6 = f32[5,1,16,256]{3,2,1,0:T(8,128)S(1)} collective-permute-done((f32[5,1,16,256]{3,2,1,0:T(8,128)S(1)}, f32[5,1,16,256]{3,2,1,0:T(8,128)S(1)}, u32[]{:S(2)}, u32[]{:S(2)}) %collective-permute-start.6) | collective-permute-done | bytes 81952 | tf_op jit(solution)/shard_map/ppermute | solution.py:78
  144.7 3.8 %collective-permute-start.8 = (f32[5,16,1,256]{3,1,2,0:T(8,128)S(1)}, f32[5,16,1,256]{3,1,2,0:T(8,128)S(1)}, u32[]{:S(2)}, u32[]{:S(2)}) collective-permute-start(f32[5,16,1,256]{3,1,2,0:T(8,128)S(1)} %constant_dynamic-update-slice_fusion.10), channel_id=1, source_target_pairs={{0,4},{4,8},{8,12},{12,0},{1,5},{5,9},{9,13},{13,1},{2,6},{6,10},{... | collective-permute-start | bytes 245768 | tf_op jit(solution)/shard_map/ppermute | solution.py:78
  152.6 5.6 %collective-permute-start.14 = (f32[3,19,1,256]{3,2,1,0:T(1,128)}, f32[3,19,1,256]{3,2,1,0:T(1,128)}, u32[]{:S(2)}, u32[]{:S(2)}) collective-permute-start(f32[3,19,1,256]{3,2,1,0:T(1,128)} %pad_maximum_fusion.19), channel_id=1, source_target_pairs={{0,4},{4,8},{8,12},{12,0},{1,5},{5,9},{9,13},{13,1},{2,6},{6,10},{... | collective-permute-start | bytes 175112 | tf_op jit(solution)/shard_map/ppermute | solution.py:46
  160.4 1.0 collective-permute-start.11
  166.9 1.5 copy.2983
  168.4 1.2 collective-permute-done.10
  169.6 1.4 slice_bitcast_fusion.33
  171.0 1.5 copy.2981
  172.5 1.5 copy.2986
  174.0 1.5 copy.2987
  175.5 1.5 copy.2988
  177.1 1.5 copy.2989
  178.6 1.5 copy.2990
  180.1 1.9 fusion.171
  181.9 1.9 fusion.172
  183.8 1.7 fusion.166
  185.5 1.5 fusion.163
  187.0 1.7 fusion.160
  189.5 0.8 fusion.154
  190.3 1.8 fusion.151
  192.1 0.9 fusion.148
  193.0 0.8 fusion.145
  193.8 0.9 fusion.142
  194.7 0.8 copy.2991
  195.5 1.1 pad_maximum_fusion
  197.0 1.0 copy.2995
  198.1 1.5 collective-permute-start.17
  200.3 1.8 fusion.139
  202.1 0.9 copy.2992
  203.0 1.8 collective-permute-done.16
  205.3 1.3 copy.2997
  206.6 13.8 %multiply_reduce_fusion = f32[3,2048]{1,0:T(4,128)S(1)} fusion(f32[19,2048]{1,0:T(8,128)S(1)} %copy-done.6, f32[19,2048]{1,0:T(8,128)S(1)} %copy-done.8, f32[3,19,19,2]{3,2,1,0:T(8,128)S(1)} %copy.2997, f32[3,19,2,256]{3,2,1,0:T(2,128)} %collective-permute-done.15, f32[3,2,16,256]{3,2,1,0:T(8,128)S(1)} %copy-done.4, ...), kind=kOutput, calls=%fused_computation | convolution fusion | flops 3461473792 | bytes 1523396 | tf_op jit(solution)/shard_map/dot_general | solution.py:209
  221.5 3.5 %all-to-all-start.2 = ((f32[16,1,384]{2,1,0:T(1,128)}), f32[16,1,384]{2,1,0:T(1,128)S(1)}, u32[]{:S(2)}, u32[]{:S(2)}) async-start(f32[16,1,384]{2,1,0:T(1,128)} %reshape.512), calls=%async_computation.2 | async-start | bytes 49152 | tf_op jit(solution)/shard_map/all_to_all | solution.py:267
  225.0 0.9 fusion.136
  226.1 5.3 %all-to-all-done.2 = f32[16,1,384]{2,1,0:T(1,128)S(1)} async-done(((f32[16,1,384]{2,1,0:T(1,128)}), f32[16,1,384]{2,1,0:T(1,128)S(1)}, u32[]{:S(2)}, u32[]{:S(2)}) %all-to-all-start.2) | async-done | bytes 24608 | tf_op jit(solution)/shard_map/all_to_all | solution.py:267
  233.0 12.1 %all-to-all-start.3 = ((f32[16,1,384]{2,1,0:T(1,128)}), f32[16,1,384]{2,1,0:T(1,128)S(1)}, u32[]{:S(2)}, u32[]{:S(2)}) async-start(f32[16,1,384]{2,1,0:T(1,128)} %reshape.514), calls=%async_computation.3 | async-start | bytes 49152 | tf_op jit(solution)/shard_map/all_to_all | solution.py:266
  245.1 0.9 fusion.133
  246.0 6.5 %all-to-all-done.3 = f32[16,1,384]{2,1,0:T(1,128)S(1)} async-done(((f32[16,1,384]{2,1,0:T(1,128)}), f32[16,1,384]{2,1,0:T(1,128)S(1)}, u32[]{:S(2)}, u32[]{:S(2)}) %all-to-all-start.3) | async-done | bytes 24608 | tf_op jit(solution)/shard_map/all_to_all | solution.py:266
  253.7 4.5 %fusion = f32[3,1024]{1,0:T(4,128)} fusion(f32[3,2048]{1,0:T(4,128)S(1)} %reshape.496, s32[1024]{0:T(1024)S(1)} %bitcast.786), kind=kOutput, calls=%fused_computation.2 | convolution fusion | flops 77594624 | bytes 40960 | tf_op jit(solution)/shard_map/dot_general | solution.py:274
  (235 shorter events, 33.7 us)
Async XLA Ops:
  2.6 4.2 %copy-start.35 = (s32[1024,1]{0,1:T(1,128)}, s32[1024,1]{0,1:T(1,128)S(1)}, u32[]{:S(2)}) copy-start(s32[1024,1]{0,1:T(1,128)S(1)} %multiply_add_fusion.3) | copy-start | bytes 12292
  43.1 18.2 %copy-start.30 = (s32[2048]{0:T(1024)}, s32[2048]{0:T(1024)S(1)}, u32[]{:S(2)}) copy-start(s32[2048]{0:T(1024)S(1)} %get-tuple-element.67) | copy-start | bytes 24580
  43.1 18.2 %copy-start.31 = (s32[2048]{0:T(1024)}, s32[2048]{0:T(1024)S(1)}, u32[]{:S(2)}) copy-start(s32[2048]{0:T(1024)S(1)} %get-tuple-element.68) | copy-start | bytes 24580
  43.1 18.2 %copy-start.32 = (s32[2048]{0:T(1024)}, s32[2048]{0:T(1024)S(1)}, u32[]{:S(2)}) copy-start(s32[2048]{0:T(1024)S(1)} %get-tuple-element.69) | copy-start | bytes 24580
  43.1 18.2 %copy-start.33 = (s32[2048]{0:T(1024)}, s32[2048]{0:T(1024)S(1)}, u32[]{:S(2)}) copy-start(s32[2048]{0:T(1024)S(1)} %get-tuple-element.70) | copy-start | bytes 24580
  44.2 0.7 copy-start.7
  44.3 6.4 %copy-start.5 = (f32[19,2048]{1,0:T(8,128)}, f32[19,2048]{1,0:T(8,128)S(1)}, u32[]{:S(2)}) copy-start(f32[19,2048]{1,0:T(8,128)S(1)} %get-tuple-element.92) | copy-start | bytes 466948
  61.3 10.6 %copy-start.25 = (f32[2048]{0:T(1024)}, f32[2048]{0:T(1024)S(1)}, u32[]{:S(2)}) copy-start(f32[2048]{0:T(1024)S(1)} %get-tuple-element.78) | copy-start | bytes 24580
  61.3 10.6 %copy-start.27 = (f32[2048]{0:T(1024)}, f32[2048]{0:T(1024)S(1)}, u32[]{:S(2)}) copy-start(f32[2048]{0:T(1024)S(1)} %get-tuple-element.79) | copy-start | bytes 24580
  61.3 10.6 %copy-start.29 = (f32[2048]{0:T(1024)}, f32[2048]{0:T(1024)S(1)}, u32[]{:S(2)}) copy-start(f32[2048]{0:T(1024)S(1)} %get-tuple-element.80) | copy-start | bytes 24580
  74.4 10.0 %collective-permute-start = (f32[3,2,19,259]{3,2,1,0:T(8,128)S(1)}, f32[3,2,19,259]{3,2,1,0:T(8,128)S(1)}, u32[]{:S(2)}, u32[]{:S(2)}) collective-permute-start(f32[3,2,19,259]{3,2,1,0:T(8,128)S(1)} %slice.626), channel_id=1, source_target_pairs={{0,16},{16,32},{32,48},{48,64},{64,80},{80,96},{96,112},{112,128},... | collective-permute-start | bytes 354320 | tf_op jit(solution)/shard_map/ppermute | solution.py:151
  75.6 6.3 %collective-permute-start.1 = (f32[3,1,19,259]{3,2,1,0:T(8,128)S(1)}, f32[3,1,19,259]{3,2,1,0:T(8,128)S(1)}, u32[]{:S(2)}, u32[]{:S(2)}) collective-permute-start(f32[3,1,19,259]{3,2,1,0:T(8,128)S(1)} %slice.627), channel_id=1, source_target_pairs={{16,0},{32,16},{48,32},{64,48},{80,64},{96,80},{112,96},{128,112},... | collective-permute-start | bytes 177164 | tf_op jit(solution)/shard_map/ppermute | solution.py:150
  86.1 11.5 %collective-permute-start.2 = (f32[3,16,2,259]{3,2,1,0:T(2,128)S(1)}, f32[3,16,2,259]{3,2,1,0:T(2,128)S(1)}, u32[]{:S(2)}, u32[]{:S(2)}) collective-permute-start(f32[3,16,2,259]{3,2,1,0:T(2,128)S(1)} %slice.629), channel_id=1, source_target_pairs={{0,4},{4,8},{8,12},{12,0},{1,5},{5,9},{9,13},{13,1},{2,6},{6,10},{... | collective-permute-start | bytes 298376 | tf_op jit(solution)/shard_map/ppermute | solution.py:151
  87.7 9.9 %collective-permute-start.3 = (f32[3,16,1,259]{3,2,1,0:T(1,128)S(1)}, f32[3,16,1,259]{3,2,1,0:T(1,128)S(1)}, u32[]{:S(2)}, u32[]{:S(2)}) collective-permute-start(f32[3,16,1,259]{3,2,1,0:T(1,128)S(1)} %slice.630), channel_id=1, source_target_pairs={{4,0},{8,4},{12,8},{0,12},{5,1},{9,5},{13,9},{1,13},{6,2},{10,6},{... | collective-permute-start | bytes 149192 | tf_op jit(solution)/shard_map/ppermute | solution.py:150
  98.0 20.6 %collective-permute-start.4 = (f32[3,16,16,2]{3,2,1,0:T(8,128)S(1)}, f32[3,16,16,2]{3,2,1,0:T(8,128)S(1)}, u32[]{:S(2)}, u32[]{:S(2)}) collective-permute-start(f32[3,16,16,2]{3,2,1,0:T(8,128)S(1)} %slice.632), channel_id=1, source_target_pairs={{0,1},{1,2},{2,3},{3,0},{4,5},{5,6},{6,7},{7,4},{8,9},{9,10},{10,1... | collective-permute-start | bytes 18440 | tf_op jit(solution)/shard_map/ppermute | solution.py:151
  99.2 19.4 %collective-permute-start.5 = (f32[3,16,16,1]{3,2,1,0:T(8,128)S(1)}, f32[3,16,16,1]{3,2,1,0:T(8,128)S(1)}, u32[]{:S(2)}, u32[]{:S(2)}) collective-permute-start(f32[3,16,16,1]{3,2,1,0:T(8,128)S(1)} %slice.633), channel_id=1, source_target_pairs={{1,0},{2,1},{3,2},{0,3},{5,4},{6,5},{7,6},{4,7},{9,8},{10,9},{11,1... | collective-permute-start | bytes 9224 | tf_op jit(solution)/shard_map/ppermute | solution.py:150
  118.6 4.5 %slice-start = ((s8[4980736]{0:T(1024)(128)(4,1)}), s8[4194304]{0:T(1024)(128)(4,1)S(1)}, s32[]{:S(2)}) async-start(s8[4980736]{0:T(1024)(128)(4,1)} %bitcast.767), calls=%async_computation.4 | async-start | bytes 8388608
  119.0 4.1 %slice-start.1 = ((s8[4980736]{0:T(1024)(128)(4,1)}), s8[786432]{0:T(1024)(128)(4,1)S(1)}, s32[]{:S(2)}) async-start(s8[4980736]{0:T(1024)(128)(4,1)} %bitcast.767), calls=%async_computation.5 | async-start | bytes 1572864
  125.4 12.6 %copy-start.2 = (f32[16,16,256]{2,1,0:T(8,128)}, f32[16,16,256]{2,1,0:T(8,128)S(1)}, u32[]{:S(2)}) copy-start(f32[16,16,256]{2,1,0:T(8,128)S(1)} %get-tuple-element.16) | copy-start | bytes 786436
  129.5 22.5 %collective-permute-start.13 = (f32[3,2,16,256]{3,2,1,0:T(8,128)S(1)}, f32[3,2,16,256]{3,2,1,0:T(8,128)S(1)}, u32[]{:S(2)}, u32[]{:S(2)}) collective-permute-start(f32[3,2,16,256]{3,2,1,0:T(8,128)S(1)} %pad_maximum_fusion.17), channel_id=1, source_target_pairs={{16,0},{32,16},{48,32},{64,48},{80,64},{96,80},{112,96},{128,112},... | collective-permute-start | bytes 294920 | tf_op jit(solution)/shard_map/ppermute | solution.py:48
  132.7 19.2 %collective-permute-start.12 = (f32[3,1,16,256]{3,2,1,0:T(8,128)S(1)}, f32[3,1,16,256]{3,2,1,0:T(8,128)S(1)}, u32[]{:S(2)}, u32[]{:S(2)}) collective-permute-start(f32[3,1,16,256]{3,2,1,0:T(8,128)S(1)} %pad_maximum_fusion.20), channel_id=1, source_target_pairs={{0,16},{16,32},{32,48},{48,64},{64,80},{80,96},{96,112},{112,128},... | collective-permute-start | bytes 147464 | tf_op jit(solution)/shard_map/ppermute | solution.py:46
  132.9 6.3 %collective-permute-start.7 = (f32[5,1,16,256]{3,2,1,0:T(8,128)S(1)}, f32[5,1,16,256]{3,2,1,0:T(8,128)S(1)}, u32[]{:S(2)}, u32[]{:S(2)}) collective-permute-start(f32[5,1,16,256]{3,2,1,0:T(8,128)S(1)} %constant_dynamic-update-slice_fusion.5), channel_id=1, source_target_pairs={{16,0},{32,16},{48,32},{64,48},{80,64},{96,80},{112,96},{128,112},... | collective-permute-start | bytes 245768 | tf_op jit(solution)/shard_map/ppermute | solution.py:79
  137.8 10.7 %copy-start.1 = (f32[15,16,256]{2,1,0:T(8,128)}, f32[15,16,256]{2,1,0:T(8,128)S(1)}, u32[]{:S(2)}) copy-start(f32[15,16,256]{2,1,0:T(8,128)S(1)} %slice.653) | copy-start | bytes 737284
  137.8 10.9 %copy-start = (f32[15,16,256]{2,1,0:T(8,128)}, f32[15,16,256]{2,1,0:T(8,128)S(1)}, u32[]{:S(2)}) copy-start(f32[15,16,256]{2,1,0:T(8,128)S(1)} %slice.665) | copy-start | bytes 737284
  137.9 6.7 %collective-permute-start.6 = (f32[5,1,16,256]{3,2,1,0:T(8,128)S(1)}, f32[5,1,16,256]{3,2,1,0:T(8,128)S(1)}, u32[]{:S(2)}, u32[]{:S(2)}) collective-permute-start(f32[5,1,16,256]{3,2,1,0:T(8,128)S(1)} %constant_dynamic-update-slice_fusion), channel_id=1, source_target_pairs={{0,16},{16,32},{32,48},{48,64},{64,80},{80,96},{96,112},{112,128},... | collective-permute-start | bytes 245768 | tf_op jit(solution)/shard_map/ppermute | solution.py:78
  139.2 12.7 %copy-start.13 = (f32[1,16,256]{2,1,0:T(8,128)}, f32[1,16,256]{2,1,0:T(8,128)S(1)}, u32[]{:S(2)}) copy-start(f32[1,16,256]{2,1,0:T(8,128)S(1)} %get-tuple-element.54) | copy-start | bytes 49156
  144.6 7.3 %copy-start.14 = (f32[1,16,256]{2,1,0:T(8,128)}, f32[1,16,256]{2,1,0:T(8,128)S(1)}, u32[]{:S(2)}) copy-start(f32[1,16,256]{2,1,0:T(8,128)S(1)} %get-tuple-element.49) | copy-start | bytes 49156
  144.6 7.3 %copy-start.15 = (f32[1,16,256]{2,1,0:T(8,128)}, f32[1,16,256]{2,1,0:T(8,128)S(1)}, u32[]{:S(2)}) copy-start(f32[1,16,256]{2,1,0:T(8,128)S(1)} %get-tuple-element.50) | copy-start | bytes 49156
  144.7 14.3 %collective-permute-start.8 = (f32[5,16,1,256]{3,1,2,0:T(8,128)S(1)}, f32[5,16,1,256]{3,1,2,0:T(8,128)S(1)}, u32[]{:S(2)}, u32[]{:S(2)}) collective-permute-start(f32[5,16,1,256]{3,1,2,0:T(8,128)S(1)} %constant_dynamic-update-slice_fusion.10), channel_id=1, source_target_pairs={{0,4},{4,8},{8,12},{12,0},{1,5},{5,9},{9,13},{13,1},{2,6},{6,10},{... | collective-permute-start | bytes 245768 | tf_op jit(solution)/shard_map/ppermute | solution.py:78
  148.5 11.1 %collective-permute-start.9 = (f32[5,16,1,256]{3,2,1,0:T(1,128)S(1)}, f32[5,16,1,256]{3,2,1,0:T(1,128)S(1)}, u32[]{:S(2)}, u32[]{:S(2)}) collective-permute-start(f32[5,16,1,256]{3,2,1,0:T(1,128)S(1)} %constant_dynamic-update-slice_fusion.15), channel_id=1, source_target_pairs={{4,0},{8,4},{12,8},{0,12},{5,1},{9,5},{13,9},{1,13},{6,2},{10,6},{... | collective-permute-start | bytes 245768 | tf_op jit(solution)/shard_map/ppermute | solution.py:79
  152.0 43.6 %copy-start.3 = (f32[3,2,16,256]{3,2,1,0:T(8,128)}, f32[3,2,16,256]{3,2,1,0:T(8,128)S(1)}, u32[]{:S(2)}) copy-start(f32[3,2,16,256]{3,2,1,0:T(8,128)S(1)} %collective-permute-done.13) | copy-start | bytes 294916
  152.6 42.9 %collective-permute-start.14 = (f32[3,19,1,256]{3,2,1,0:T(1,128)}, f32[3,19,1,256]{3,2,1,0:T(1,128)}, u32[]{:S(2)}, u32[]{:S(2)}) collective-permute-start(f32[3,19,1,256]{3,2,1,0:T(1,128)} %pad_maximum_fusion.19), channel_id=1, source_target_pairs={{0,4},{4,8},{8,12},{12,0},{1,5},{5,9},{9,13},{13,1},{2,6},{6,10},{... | collective-permute-start | bytes 175112 | tf_op jit(solution)/shard_map/ppermute | solution.py:46
  158.9 36.6 %collective-permute-start.15 = (f32[3,19,2,256]{3,2,1,0:T(2,128)}, f32[3,19,2,256]{3,2,1,0:T(2,128)}, u32[]{:S(2)}, u32[]{:S(2)}) collective-permute-start(f32[3,19,2,256]{3,2,1,0:T(2,128)} %pad_maximum_fusion.13), channel_id=1, source_target_pairs={{4,0},{8,4},{12,8},{0,12},{5,1},{9,5},{13,9},{1,13},{6,2},{10,6},{... | collective-permute-start | bytes 350216 | tf_op jit(solution)/shard_map/ppermute | solution.py:48
  159.0 0.6 copy-start.20
  160.2 4.8 %copy-start.16 = (f32[16,1,256]{2,1,0:T(1,128)}, f32[16,1,256]{2,1,0:T(1,128)S(1)}, u32[]{:S(2)}) copy-start(f32[16,1,256]{2,1,0:T(1,128)S(1)} %get-tuple-element.45) | copy-start | bytes 49156
  160.2 4.8 %copy-start.18 = (f32[16,1,256]{2,1,0:T(1,128)}, f32[16,1,256]{2,1,0:T(1,128)S(1)}, u32[]{:S(2)}) copy-start(f32[16,1,256]{2,1,0:T(1,128)S(1)} %get-tuple-element.44) | copy-start | bytes 49156
  160.4 5.9 %collective-permute-start.11 = (f32[5,16,16,1]{2,1,3,0:T(8,128)S(1)}, f32[5,16,16,1]{2,1,3,0:T(8,128)S(1)}, u32[]{:S(2)}, u32[]{:S(2)}) collective-permute-start(f32[5,16,16,1]{2,1,3,0:T(8,128)S(1)} %constant_dynamic-update-slice_fusion.25), channel_id=1, source_target_pairs={{1,0},{2,1},{3,2},{0,3},{5,4},{6,5},{7,6},{4,7},{9,8},{10,9},{11,1... | collective-permute-start | bytes 15368 | tf_op jit(solution)/shard_map/ppermute | solution.py:79
  161.4 4.3 %copy-start.22 = (f32[16,1,256]{2,1,0:T(1,128)}, f32[16,1,256]{2,1,0:T(1,128)S(1)}, u32[]{:S(2)}) copy-start(f32[16,1,256]{2,1,0:T(1,128)S(1)} %copy.2980) | copy-start | bytes 49156
  163.0 6.7 %collective-permute-start.10 = (f32[5,16,16,1]{2,1,3,0:T(8,128)}, f32[5,16,16,1]{2,1,3,0:T(8,128)}, u32[]{:S(2)}, u32[]{:S(2)}) collective-permute-start(f32[5,16,16,1]{2,1,3,0:T(8,128)} %constant_dynamic-update-slice_fusion.20), channel_id=1, source_target_pairs={{0,1},{1,2},{2,3},{3,0},{4,5},{5,6},{6,7},{7,4},{8,9},{9,10},{10,1... | collective-permute-start | bytes 15368 | tf_op jit(solution)/shard_map/ppermute | solution.py:78
  180.1 8.7 %copy-start.24 = (f32[16,1,256]{2,1,0:T(1,128)S(1)}, f32[16,1,256]{2,1,0:T(1,128)}, u32[]{:S(2)}) copy-start(f32[16,1,256]{2,1,0:T(1,128)} %copy.2985) | copy-start | bytes 49156
  180.1 9.4 %copy-start.11 = (f32[16,16,1]{2,1,0:T(8,128)S(1)}, f32[16,16,1]{2,1,0:T(8,128)}, u32[]{:S(2)}) copy-start(f32[16,16,1]{2,1,0:T(8,128)} %copy.2986) | copy-start | bytes 3076
  181.9 10.2 %copy-start.10 = (f32[16,16,1]{2,1,0:T(8,128)S(1)}, f32[16,16,1]{2,1,0:T(8,128)}, u32[]{:S(2)}) copy-start(f32[16,16,1]{2,1,0:T(8,128)} %copy.2988) | copy-start | bytes 3076
  183.8 9.2 %copy-start.9 = (f32[16,16,1]{2,1,0:T(8,128)S(1)}, f32[16,16,1]{2,1,0:T(8,128)}, u32[]{:S(2)}) copy-start(f32[16,16,1]{2,1,0:T(8,128)} %copy.2989) | copy-start | bytes 3076
  185.5 8.3 %copy-start.12 = (f32[16,16,1]{2,1,0:T(8,128)S(1)}, f32[16,16,1]{2,1,0:T(8,128)}, u32[]{:S(2)}) copy-start(f32[16,16,1]{2,1,0:T(8,128)} %copy.2990) | copy-start | bytes 3076
  185.5 8.3 %copy-start.23 = (f32[16,1,256]{2,1,0:T(1,128)S(1)}, f32[16,1,256]{2,1,0:T(1,128)}, u32[]{:S(2)}) copy-start(f32[16,1,256]{2,1,0:T(1,128)} %copy-done.22) | copy-start | bytes 49156
  196.6 3.6 %copy-start.19 = (f32[16,1,256]{2,1,0:T(1,128)S(1)}, f32[16,1,256]{2,1,0:T(1,128)}, u32[]{:S(2)}) copy-start(f32[16,1,256]{2,1,0:T(1,128)} %copy-done.18) | copy-start | bytes 49156
  197.0 9.6 %copy-start.4 = (f32[3,2,16,256]{3,2,1,0:T(8,128)S(1)}, f32[3,2,16,256]{3,2,1,0:T(8,128)}, u32[]{:S(2)}) copy-start(f32[3,2,16,256]{3,2,1,0:T(8,128)} %copy-done.3) | copy-start | bytes 294916
  197.0 9.6 %copy-start.6 = (f32[19,2048]{1,0:T(8,128)S(1)}, f32[19,2048]{1,0:T(8,128)}, u32[]{:S(2)}) copy-start(f32[19,2048]{1,0:T(8,128)} %copy-done.5) | copy-start | bytes 466948
  197.0 9.6 %copy-start.8 = (f32[19,2048]{1,0:T(8,128)S(1)}, f32[19,2048]{1,0:T(8,128)}, u32[]{:S(2)}) copy-start(f32[19,2048]{1,0:T(8,128)} %copy-done.7) | copy-start | bytes 466948
  197.0 9.6 %copy-start.26 = (f32[2048]{0:T(1024)S(1)}, f32[2048]{0:T(1024)}, u32[]{:S(2)}) copy-start(f32[2048]{0:T(1024)} %copy-done.25) | copy-start | bytes 24580
  197.0 9.6 %copy-start.28 = (f32[2048]{0:T(1024)S(1)}, f32[2048]{0:T(1024)}, u32[]{:S(2)}) copy-start(f32[2048]{0:T(1024)} %copy-done.27) | copy-start | bytes 24580
  198.1 7.2 %collective-permute-start.17 = (f32[3,19,19,2]{2,3,1,0:T(2,128)}, f32[3,19,19,2]{2,3,1,0:T(2,128)}, u32[]{:S(2)}, u32[]{:S(2)}) collective-permute-start(f32[3,19,19,2]{2,3,1,0:T(2,128)} %copy.2995), channel_id=1, source_target_pairs={{1,0},{2,1},{3,2},{0,3},{5,4},{6,5},{7,6},{4,7},{9,8},{10,9},{11,1... | collective-permute-start | bytes 26000 | tf_op jit(solution)/shard_map/ppermute | solution.py:48
  200.0 4.8 %collective-permute-start.16 = (f32[3,19,19,1]{2,3,1,0:T(1,128)S(1)}, f32[3,19,19,1]{2,3,1,0:T(1,128)S(1)}, u32[]{:S(2)}, u32[]{:S(2)}) collective-permute-start(f32[3,19,19,1]{2,3,1,0:T(1,128)S(1)} %copy.2994), channel_id=1, source_target_pairs={{0,1},{1,2},{2,3},{3,0},{4,5},{5,6},{6,7},{7,4},{8,9},{9,10},{10,1... | collective-permute-start | bytes 13004 | tf_op jit(solution)/shard_map/ppermute | solution.py:46
  206.6 18.4 %copy-start.21 = (f32[16,1,256]{2,1,0:T(1,128)S(1)}, f32[16,1,256]{2,1,0:T(1,128)}, u32[]{:S(2)}) copy-start(f32[16,1,256]{2,1,0:T(1,128)} %copy-done.20) | copy-start | bytes 49156
  206.6 19.4 %copy-start.34 = (f32[16,16,1]{1,0,2:T(8,128)S(1)}, f32[16,16,1]{1,0,2:T(8,128)}, u32[]{:S(2)}) copy-start(f32[16,16,1]{1,0,2:T(8,128)} %get-tuple-element.57) | copy-start | bytes 3076
  220.4 24.8 %copy-start.17 = (f32[16,1,256]{2,1,0:T(1,128)S(1)}, f32[16,1,256]{2,1,0:T(1,128)}, u32[]{:S(2)}) copy-start(f32[16,1,256]{2,1,0:T(1,128)} %copy-done.16) | copy-start | bytes 49156
  220.6 33.1 %copy-start.36 = (s32[1024,1]{0,1:T(1,128)S(1)}, s32[1024,1]{0,1:T(1,128)}, u32[]{:S(2)}) copy-start(s32[1024,1]{0,1:T(1,128)} %copy-done.35) | copy-start | bytes 12292
  221.5 9.9 %all-to-all-start.2 = ((f32[16,1,384]{2,1,0:T(1,128)}), f32[16,1,384]{2,1,0:T(1,128)S(1)}, u32[]{:S(2)}, u32[]{:S(2)}) async-start(f32[16,1,384]{2,1,0:T(1,128)} %reshape.512), calls=%async_computation.2 | async-start | bytes 49152 | tf_op jit(solution)/shard_map/all_to_all | solution.py:267
  233.0 19.4 %all-to-all-start.3 = ((f32[16,1,384]{2,1,0:T(1,128)}), f32[16,1,384]{2,1,0:T(1,128)S(1)}, u32[]{:S(2)}, u32[]{:S(2)}) async-start(f32[16,1,384]{2,1,0:T(1,128)} %reshape.514), calls=%async_computation.3 | async-start | bytes 49152 | tf_op jit(solution)/shard_map/all_to_all | solution.py:266

commit v2 on v0

--- a/solution.py
+++ b/solution.py
@@ -221,10 +221,10 @@
     buckets = jnp.dot(record, placing, precision=highest, preferred_element_type=jnp.float32)
     buckets = buckets.reshape(7, count_first, count_rest, capacity)
     received = lax.all_to_all(
-        lax.all_to_all(buckets, "gx", split_axis=1, concat_axis=1, tiled=True),
-        ("gy", "gz"),
-        split_axis=2,
-        concat_axis=2,
+        lax.all_to_all(buckets, ("gy", "gz"), split_axis=2, concat_axis=2, tiled=True),
+        "gx",
+        split_axis=1,
+        concat_axis=1,
         tiled=True,
     )
     received = received.reshape(7, slot_count)
@@ -249,10 +249,10 @@
     sampled = sample_banded(velocity_ext, coordinates, weights, halo_sizes)
     sampled = sampled.reshape(3, count_first, count_rest, capacity)
     returned = lax.all_to_all(
-        lax.all_to_all(sampled, "gx", split_axis=1, concat_axis=1, tiled=True),
-        ("gy", "gz"),
-        split_axis=2,
-        concat_axis=2,
+        lax.all_to_all(sampled, ("gy", "gz"), split_axis=2, concat_axis=2, tiled=True),
+        "gx",
+        split_axis=1,
+        concat_axis=1,
         tiled=True,
     )
     returned = returned.reshape(3, slot_count)

time: 257 us -> 256 us (level)
  no operation moved by 1% of the time
where the time goes in v2:
time: 256 us; the launch traced here: 251 us
  other arithmetic  54.6 us (21%)
  starting transfers between devices  48.8 us (19%)
  waiting for transfers between devices  44 us (17%)
  local copies, waits for them, and re-layouts  37.9 us (15%)
  matrix products  32.9 us (13%)
  blocking collectives  30.7 us (12%)
    unnamed x21, other arithmetic  24.6 us
    ppermute x3, waiting for transfers between devices, fold_ghost(): lax.ppermute(below, axis, [((i + 1) % count, i) for i in range(count)])  24.3 us
    all_to_all x1, blocking collectives, shards(): lax.all_to_all(buckets, ('gy', 'gz'), split_axis=2, concat_axis=2, tiled=...  17.2 us
    dot_general x1, matrix products, sample_banded(): jnp.dot(flat_velocity, band_third.T, precision=three_pass, preferred_elem...  15.1 us
    all_to_all x1, blocking collectives, shards(): lax.all_to_all(lax.all_to_all(buckets, ('gy', 'gz'), split_axis=2, concat...  13.5 us
    all_to_all x1, starting transfers between devices, shards(): lax.all_to_all(sampled, ('gy', 'gz'), split_axis=2, concat_axis=2, tiled=...  12.3 us
    mul x2, local copies, waits for them, and re-layouts, spread_banded(): forces[:, None, None, :] * band_first.T[None, :, None, :]  10.6 us
    dot_general x1, matrix products, spread_banded(): jnp.dot(partial_value, band_third, precision=three_pass, preferred_elemen...  9.81 us
  transfers between devices with their start and end apart: 20, of which 9 were waited for; matrix products, arithmetic and copies ran while one was open for 17% of the time, Pallas kernels for 0%

profile of v2, /device:TPU:1, one launch (start us, length us, event | category | flops | bytes accessed | tf_op | source)
XLA Modules:
  0.0 251.0 jit_solution(2573588321338710269)
XLA Ops:
  0.6 1.3 convert_reduce_fusion
  3.3 3.5 %fusion.1 = f32[7,2048]{1,0:T(8,128)S(1)} fusion(s32[1024]{0:T(1024)S(1)} %bitcast.785, f32[1,1024]{1,0:T(1,128)S(1)} %bitcast.788, f32[3,1024]{1,0:T(4,128)} %param.6, f32[3,1024]{1,0:T(4,128)} %param.7), kind=kOutput, calls=%fused_computation.3 | convolution fusion | flops 178272256 | bytes 90112 | tf_op jit(solution)/shard_map/dot_general | solution.py:221
  8.0 17.2 %all_to_all.20 = f32[16,1,896]{2,1,0:T(1,128)S(1)} all-to-all(f32[16,1,896]{2,1,0:T(1,128)S(1)} %reshape.855), channel_id=1, replica_groups=mesh['gx'=16,'gy'=4,'gz'=4] {'gy','gz'}, dimensions={0} | all-to-all | bytes 114688 | tf_op jit(solution)/shard_map/all_to_all | solution.py:224
  27.1 13.5 %all_to_all.21 = f32[16,1,896]{2,1,0:T(1,128)S(1)} all-to-all(f32[16,1,896]{2,1,0:T(1,128)S(1)} %reshape.857), channel_id=1, replica_groups=mesh['gx'=16,'gy'=4,'gz'=4] {'gx'}, dimensions={0} | all-to-all | bytes 114688 | tf_op jit(solution)/shard_map/all_to_all | solution.py:223
  43.6 5.7 %broadcast_multiply_fusion = f32[3,19,19,2048]{3,2,1,0:T(8,128)} fusion(f32[19,2048]{1,0:T(8,128)S(1)} %get-tuple-element.102, f32[3,19,2048]{2,1,0:T(8,128)S(1)} %broadcast_multiply_fusion.1), kind=kLoop, calls=%fused_computation.4 | loop fusion | flops 2217984 | bytes 9494528 | tf_op jit(solution)/shard_map/mul | solution.py:176
  49.2 10.4 %mul.1160 = f32[1083,2048]{1,0:T(8,128)} reshape(f32[3,19,19,2048]{3,2,1,0:T(8,128)} %broadcast_multiply_fusion) | data formatting | bytes 17743872 | tf_op jit(solution)/shard_map/mul | solution.py:176
  60.5 2.3 select_add_fusion
  62.8 9.8 %fusion.319 = f32[1083,259]{1,0:T(8,128)S(1)} fusion(f32[1083,2048]{1,0:T(8,128)} %mul.1160, f32[2048,259]{1,0:T(8,128)S(1)} %select_add_fusion), kind=kOutput, calls=%fused_computation.633 | convolution fusion | flops 3446747136 | bytes 12115652 | tf_op jit(solution)/shard_map/dot_general | solution.py:182
  72.6 1.5 reshape.841
  74.2 1.0 slice.626
  75.6 0.9 slice.627
  76.5 4.4 %collective-permute-start.1 = (f32[3,1,19,259]{3,2,1,0:T(8,128)S(1)}, f32[3,1,19,259]{3,2,1,0:T(8,128)S(1)}, u32[]{:S(2)}, u32[]{:S(2)}) collective-permute-start(f32[3,1,19,259]{3,2,1,0:T(8,128)S(1)} %slice.627), channel_id=1, source_target_pairs={{16,0},{32,16},{48,32},{64,48},{80,64},{96,80},{112,96},{128,112},... | collective-permute-start | bytes 177164 | tf_op jit(solution)/shard_map/ppermute | solution.py:134
  80.9 1.8 collective-permute-done.1
  82.7 1.0 collective-permute-done
  83.7 1.6 fusion.30
  85.4 3.3 %collective-permute-start.2 = (f32[3,16,2,259]{3,2,1,0:T(2,128)S(1)}, f32[3,16,2,259]{3,2,1,0:T(2,128)S(1)}, u32[]{:S(2)}, u32[]{:S(2)}) collective-permute-start(f32[3,16,2,259]{3,2,1,0:T(2,128)S(1)} %slice.629), channel_id=1, source_target_pairs={{0,4},{4,8},{8,12},{12,0},{1,5},{5,9},{9,13},{13,1},{2,6},{6,10},{... | collective-permute-start | bytes 298376 | tf_op jit(solution)/shard_map/ppermute | solution.py:135
  88.9 3.0 %reduce_sum.31 = f32[16,16,256]{2,1,0:T(8,128)S(1)} reduce(f32[19,16,16,256]{3,2,1,0:T(8,128)} %param.5, f32[]{:T(128)} %constant.146.clone.1), dimensions={0}, to_apply=%region_0.0 | reduce | flops 1179648 | bytes 5242884 | tf_op jit(solution)/shard_map/reduce_sum | solution.py:87
  91.9 6.4 %collective-permute-done.3 = f32[3,16,1,259]{3,2,1,0:T(1,128)S(1)} collective-permute-done((f32[3,16,1,259]{3,2,1,0:T(1,128)S(1)}, f32[3,16,1,259]{3,2,1,0:T(1,128)S(1)}, u32[]{:S(2)}, u32[]{:S(2)}) %collective-permute-start.3) | collective-permute-done | bytes 49760 | tf_op jit(solution)/shard_map/ppermute | solution.py:134
  98.7 1.2 collective-permute-start.4
  100.0 2.3 collective-permute-start.5
  102.3 0.9 select_add_fusion.1
  103.2 16.1 %collective-permute-done.5 = f32[3,16,16,1]{3,2,1,0:T(8,128)S(1)} collective-permute-done((f32[3,16,16,1]{3,2,1,0:T(8,128)S(1)}, f32[3,16,16,1]{3,2,1,0:T(8,128)S(1)}, u32[]{:S(2)}, u32[]{:S(2)}) %collective-permute-start.5) | collective-permute-done | bytes 3104 | tf_op jit(solution)/shard_map/ppermute | solution.py:134
  119.7 3.8 %fusion.279 = (f32[19,16,16,256]{3,2,1,0:T(8,128)}, f32[1,16,16,256]{3,2,1,0:T(8,128)S(1)}, f32[1,16,16,256]{3,2,1,0:T(8,128)S(1)}, f32[1,16,16,256]{3,2,1,0:T(8,128)S(1)}) fusion(f32[16,16,256]{2,1,0:T(8,128)S(1)} %reduce_sum.31, f32[19,16,16,256]{3,2,1,0:T(8,128)} %param.5, f32[3,16,16,256]{3,2,1,0:T(8,128)S(1)} %fusion.41), kind=kLoop, calls=%fused_computation.434 | loop fusion | flops 4784127 | bytes 7077888
  125.9 0.8 fusion.118
  126.7 0.8 fusion.132
  128.0 0.8 fusion.104
  129.1 0.8 slice.688
  130.0 4.8 %collective-permute-start.13 = (f32[3,2,16,256]{3,2,1,0:T(8,128)S(1)}, f32[3,2,16,256]{3,2,1,0:T(8,128)S(1)}, u32[]{:S(2)}, u32[]{:S(2)}) collective-permute-start(f32[3,2,16,256]{3,2,1,0:T(8,128)S(1)} %get-tuple-element.38), channel_id=1, source_target_pairs={{16,0},{32,16},{48,32},{64,48},{80,64},{96,80},{112,96},{128,112},... | collective-permute-start | bytes 294920 | tf_op jit(solution)/shard_map/ppermute | solution.py:48
  134.9 1.4 collective-permute-start.7
  138.4 4.8 %collective-permute-done.6 = f32[5,1,16,256]{3,2,1,0:T(8,128)S(1)} collective-permute-done((f32[5,1,16,256]{3,2,1,0:T(8,128)S(1)}, f32[5,1,16,256]{3,2,1,0:T(8,128)S(1)}, u32[]{:S(2)}, u32[]{:S(2)}) %collective-permute-start.6) | collective-permute-done | bytes 81952 | tf_op jit(solution)/shard_map/ppermute | solution.py:62
  143.3 3.8 %collective-permute-start.8 = (f32[5,16,1,256]{3,1,2,0:T(8,128)S(1)}, f32[5,16,1,256]{3,1,2,0:T(8,128)S(1)}, u32[]{:S(2)}, u32[]{:S(2)}) collective-permute-start(f32[5,16,1,256]{3,1,2,0:T(8,128)S(1)} %constant_dynamic-update-slice_fusion.10), channel_id=1, source_target_pairs={{0,4},{4,8},{8,12},{12,0},{1,5},{5,9},{9,13},{13,1},{2,6},{6,10},{... | collective-permute-start | bytes 245768 | tf_op jit(solution)/shard_map/ppermute | solution.py:62
  150.6 0.8 pad_maximum_fusion.17
  151.4 5.6 %collective-permute-start.14 = (f32[3,20,2,256]{3,2,1,0:T(2,128)}, f32[3,20,2,256]{3,2,1,0:T(2,128)}, u32[]{:S(2)}, u32[]{:S(2)}) collective-permute-start(f32[3,20,2,256]{3,2,1,0:T(2,128)} %get-tuple-element.35), channel_id=1, source_target_pairs={{0,4},{4,8},{8,12},{12,0},{1,5},{5,9},{9,13},{13,1},{2,6},{6,10},{... | collective-permute-start | bytes 368648 | tf_op jit(solution)/shard_map/ppermute | solution.py:46
  158.4 1.0 collective-permute-start.11
  165.0 0.8 copy.2983
  165.8 1.4 collective-permute-done.10
  167.2 1.4 slice_bitcast_fusion.33
  168.6 0.8 copy.2981
  169.4 0.8 copy.2986
  170.2 0.8 copy.2987
  171.0 0.9 copy.2988
  171.9 0.9 copy.2989
  172.8 1.9 fusion.187
  174.6 1.8 fusion.188
  176.4 1.7 fusion.182
  178.1 1.5 fusion.179
  179.6 1.7 fusion.176
  181.3 1.5 fusion.173
  182.8 1.8 fusion.170
  184.6 0.9 fusion.167
  185.4 0.9 fusion.164
  186.3 0.8 fusion.161
  187.5 1.6 fusion.158
  189.1 1.2 pad_maximum_fusion
  191.7 3.6 %collective-permute-start.17 = (f32[3,20,20,2]{2,3,1,0:T(2,128)S(1)}, f32[3,20,20,2]{2,3,1,0:T(2,128)S(1)}, u32[]{:S(2)}, u32[]{:S(2)}) collective-permute-start(f32[3,20,20,2]{2,3,1,0:T(2,128)S(1)} %copy.2995), channel_id=1, source_target_pairs={{1,0},{2,1},{3,2},{0,3},{5,4},{6,5},{7,6},{4,7},{9,8},{10,9},{11,1... | collective-permute-start | bytes 28808 | tf_op jit(solution)/shard_map/ppermute | solution.py:48
  195.3 0.9 fusion.155
  197.4 15.1 %multiply_reduce_fusion = f32[3,2048]{1,0:T(4,128)S(1)} fusion(f32[20,2048]{1,0:T(8,128)} %get-tuple-element.100, f32[20,2048]{1,0:T(8,128)} %get-tuple-element.101, f32[3,20,20,2]{3,2,1,0:T(8,128)S(1)} %copy.2997, f32[3,20,2,256]{3,2,1,0:T(2,128)} %collective-permute-done.15, f32[3,2,16,256]{3,2,1,0:T(8,128)S(1)} %copy-done.9, ...), kind=kOutput, calls=%fused_computation | convolution fusion | flops 3849575936 | bytes 1665792 | tf_op jit(solution)/shard_map/dot_general | solution.py:193
  213.7 12.3 %all-to-all-start.2 = ((f32[16,1,384]{2,1,0:T(1,128)}), f32[16,1,384]{2,1,0:T(1,128)S(1)}, u32[]{:S(2)}, u32[]{:S(2)}) async-start(f32[16,1,384]{2,1,0:T(1,128)} %reshape.859), calls=%async_computation.2 | async-start | bytes 49152 | tf_op jit(solution)/shard_map/all_to_all | solution.py:252
  226.0 0.9 fusion.152
  227.0 6.3 %all-to-all-done.2 = f32[16,1,384]{2,1,0:T(1,128)S(1)} async-done(((f32[16,1,384]{2,1,0:T(1,128)}), f32[16,1,384]{2,1,0:T(1,128)S(1)}, u32[]{:S(2)}, u32[]{:S(2)}) %all-to-all-start.2) | async-done | bytes 24608 | tf_op jit(solution)/shard_map/all_to_all | solution.py:252
  235.0 3.5 %all-to-all-start.3 = ((f32[16,1,384]{2,1,0:T(1,128)}), f32[16,1,384]{2,1,0:T(1,128)S(1)}, u32[]{:S(2)}, u32[]{:S(2)}) async-start(f32[16,1,384]{2,1,0:T(1,128)} %reshape.861), calls=%async_computation.3 | async-start | bytes 49152 | tf_op jit(solution)/shard_map/all_to_all | solution.py:251
  238.5 0.9 fusion.149
  239.4 5.5 %all-to-all-done.3 = f32[16,1,384]{2,1,0:T(1,128)S(1)} async-done(((f32[16,1,384]{2,1,0:T(1,128)}), f32[16,1,384]{2,1,0:T(1,128)S(1)}, u32[]{:S(2)}, u32[]{:S(2)}) %all-to-all-start.3) | async-done | bytes 24608 | tf_op jit(solution)/shard_map/all_to_all | solution.py:251
  246.1 4.5 %fusion = f32[3,1024]{1,0:T(4,128)} fusion(f32[3,2048]{1,0:T(4,128)S(1)} %reshape.843, s32[1024]{0:T(1024)S(1)} %bitcast.786), kind=kOutput, calls=%fused_computation.2 | convolution fusion | flops 77594624 | bytes 40960 | tf_op jit(solution)/shard_map/dot_general | solution.py:259
  (225 shorter events, 32.0 us)
Async XLA Ops:
  2.6 0.7 copy-start.31
  42.4 17.5 %copy-start.24 = (s32[2048]{0:T(1024)}, s32[2048]{0:T(1024)S(1)}, u32[]{:S(2)}) copy-start(s32[2048]{0:T(1024)S(1)} %get-tuple-element.74) | copy-start | bytes 24580
  42.4 17.5 %copy-start.25 = (s32[2048]{0:T(1024)}, s32[2048]{0:T(1024)S(1)}, u32[]{:S(2)}) copy-start(s32[2048]{0:T(1024)S(1)} %get-tuple-element.75) | copy-start | bytes 24580
  42.5 17.5 %copy-start.26 = (s32[2048]{0:T(1024)}, s32[2048]{0:T(1024)S(1)}, u32[]{:S(2)}) copy-start(s32[2048]{0:T(1024)S(1)} %get-tuple-element.76) | copy-start | bytes 24580
  59.9 0.6 copy-start.17
  59.9 0.6 copy-start.19
  59.9 0.6 copy-start.21
  59.9 0.6 copy-start.23
  75.1 8.6 %collective-permute-start = (f32[3,2,19,259]{3,2,1,0:T(8,128)S(1)}, f32[3,2,19,259]{3,2,1,0:T(8,128)S(1)}, u32[]{:S(2)}, u32[]{:S(2)}) collective-permute-start(f32[3,2,19,259]{3,2,1,0:T(8,128)S(1)} %slice.626), channel_id=1, source_target_pairs={{0,16},{16,32},{32,48},{48,64},{64,80},{80,96},{96,112},{112,128},... | collective-permute-start | bytes 354320 | tf_op jit(solution)/shard_map/ppermute | solution.py:135
  76.5 6.1 %collective-permute-start.1 = (f32[3,1,19,259]{3,2,1,0:T(8,128)S(1)}, f32[3,1,19,259]{3,2,1,0:T(8,128)S(1)}, u32[]{:S(2)}, u32[]{:S(2)}) collective-permute-start(f32[3,1,19,259]{3,2,1,0:T(8,128)S(1)} %slice.627), channel_id=1, source_target_pairs={{16,0},{32,16},{48,32},{64,48},{80,64},{96,80},{112,96},{128,112},... | collective-permute-start | bytes 177164 | tf_op jit(solution)/shard_map/ppermute | solution.py:134
  85.4 12.9 %collective-permute-start.2 = (f32[3,16,2,259]{3,2,1,0:T(2,128)S(1)}, f32[3,16,2,259]{3,2,1,0:T(2,128)S(1)}, u32[]{:S(2)}, u32[]{:S(2)}) collective-permute-start(f32[3,16,2,259]{3,2,1,0:T(2,128)S(1)} %slice.629), channel_id=1, source_target_pairs={{0,4},{4,8},{8,12},{12,0},{1,5},{5,9},{9,13},{13,1},{2,6},{6,10},{... | collective-permute-start | bytes 298376 | tf_op jit(solution)/shard_map/ppermute | solution.py:135
  88.8 9.5 %collective-permute-start.3 = (f32[3,16,1,259]{3,2,1,0:T(1,128)S(1)}, f32[3,16,1,259]{3,2,1,0:T(1,128)S(1)}, u32[]{:S(2)}, u32[]{:S(2)}) collective-permute-start(f32[3,16,1,259]{3,2,1,0:T(1,128)S(1)} %slice.630), channel_id=1, source_target_pairs={{4,0},{8,4},{12,8},{0,12},{5,1},{9,5},{13,9},{1,13},{6,2},{10,6},{... | collective-permute-start | bytes 149192 | tf_op jit(solution)/shard_map/ppermute | solution.py:134
  88.8 34.7 %slice-start = ((s8[4980736]{0:T(1024)(128)(4,1)}), s8[786432]{0:T(1024)(128)(4,1)S(1)}, s32[]{:S(2)}) async-start(s8[4980736]{0:T(1024)(128)(4,1)} %bitcast.767), calls=%async_computation.4 | async-start | bytes 1572864
  98.7 20.6 %collective-permute-start.4 = (f32[3,16,16,2]{3,2,1,0:T(8,128)S(1)}, f32[3,16,16,2]{3,2,1,0:T(8,128)S(1)}, u32[]{:S(2)}, u32[]{:S(2)}) collective-permute-start(f32[3,16,16,2]{3,2,1,0:T(8,128)S(1)} %slice.632), channel_id=1, source_target_pairs={{0,1},{1,2},{2,3},{3,0},{4,5},{5,6},{6,7},{7,4},{8,9},{9,10},{10,1... | collective-permute-start | bytes 18440 | tf_op jit(solution)/shard_map/ppermute | solution.py:135
  100.0 19.3 %collective-permute-start.5 = (f32[3,16,16,1]{3,2,1,0:T(8,128)S(1)}, f32[3,16,16,1]{3,2,1,0:T(8,128)S(1)}, u32[]{:S(2)}, u32[]{:S(2)}) collective-permute-start(f32[3,16,16,1]{3,2,1,0:T(8,128)S(1)} %slice.633), channel_id=1, source_target_pairs={{1,0},{2,1},{3,2},{0,3},{5,4},{6,5},{7,6},{4,7},{9,8},{10,9},{11,1... | collective-permute-start | bytes 9224 | tf_op jit(solution)/shard_map/ppermute | solution.py:134
  102.3 21.3 %slice-start.1 = ((s8[4980736]{0:T(1024)(128)(4,1)}), s8[4194304]{0:T(1024)(128)(4,1)S(1)}, s32[]{:S(2)}) async-start(s8[4980736]{0:T(1024)(128)(4,1)} %bitcast.767), calls=%async_computation.5 | async-start | bytes 8388608
  125.9 10.9 %copy-start.3 = (f32[16,16,256]{2,1,0:T(8,128)}, f32[16,16,256]{2,1,0:T(8,128)S(1)}, u32[]{:S(2)}) copy-start(f32[16,16,256]{2,1,0:T(8,128)S(1)} %get-tuple-element.16) | copy-start | bytes 786436
  129.9 20.6 %collective-permute-start.12 = (f32[3,2,16,256]{3,2,1,0:T(8,128)S(1)}, f32[3,2,16,256]{3,2,1,0:T(8,128)S(1)}, u32[]{:S(2)}, u32[]{:S(2)}) collective-permute-start(f32[3,2,16,256]{3,2,1,0:T(8,128)S(1)} %get-tuple-element.37), channel_id=1, source_target_pairs={{0,16},{16,32},{32,48},{48,64},{64,80},{80,96},{96,112},{112,128},... | collective-permute-start | bytes 294920 | tf_op jit(solution)/shard_map/ppermute | solution.py:46
  130.0 20.6 %collective-permute-start.13 = (f32[3,2,16,256]{3,2,1,0:T(8,128)S(1)}, f32[3,2,16,256]{3,2,1,0:T(8,128)S(1)}, u32[]{:S(2)}, u32[]{:S(2)}) collective-permute-start(f32[3,2,16,256]{3,2,1,0:T(8,128)S(1)} %get-tuple-element.38), channel_id=1, source_target_pairs={{16,0},{32,16},{48,32},{64,48},{80,64},{96,80},{112,96},{128,112},... | collective-permute-start | bytes 294920 | tf_op jit(solution)/shard_map/ppermute | solution.py:48
  134.9 3.4 %collective-permute-start.7 = (f32[5,1,16,256]{3,2,1,0:T(8,128)S(1)}, f32[5,1,16,256]{3,2,1,0:T(8,128)S(1)}, u32[]{:S(2)}, u32[]{:S(2)}) collective-permute-start(f32[5,1,16,256]{3,2,1,0:T(8,128)S(1)} %constant_dynamic-update-slice_fusion.5), channel_id=1, source_target_pairs={{16,0},{32,16},{48,32},{64,48},{80,64},{96,80},{112,96},{128,112},... | collective-permute-start | bytes 245768 | tf_op jit(solution)/shard_map/ppermute | solution.py:63
  136.4 14.2 %copy-start.2 = (f32[15,16,256]{2,1,0:T(8,128)}, f32[15,16,256]{2,1,0:T(8,128)S(1)}, u32[]{:S(2)}) copy-start(f32[15,16,256]{2,1,0:T(8,128)S(1)} %slice.653) | copy-start | bytes 737284
  136.4 11.5 %copy-start.1 = (f32[15,16,256]{2,1,0:T(8,128)}, f32[15,16,256]{2,1,0:T(8,128)S(1)}, u32[]{:S(2)}) copy-start(f32[15,16,256]{2,1,0:T(8,128)S(1)} %slice.665) | copy-start | bytes 737284
  136.4 11.3 %copy-start = (f32[15,16,256]{2,1,0:T(8,128)}, f32[15,16,256]{2,1,0:T(8,128)S(1)}, u32[]{:S(2)}) copy-start(f32[15,16,256]{2,1,0:T(8,128)S(1)} %slice.671) | copy-start | bytes 737284
  136.5 6.7 %collective-permute-start.6 = (f32[5,1,16,256]{3,2,1,0:T(8,128)S(1)}, f32[5,1,16,256]{3,2,1,0:T(8,128)S(1)}, u32[]{:S(2)}, u32[]{:S(2)}) collective-permute-start(f32[5,1,16,256]{3,2,1,0:T(8,128)S(1)} %constant_dynamic-update-slice_fusion), channel_id=1, source_target_pairs={{0,16},{16,32},{32,48},{48,64},{64,80},{80,96},{96,112},{112,128},... | collective-permute-start | bytes 245768 | tf_op jit(solution)/shard_map/ppermute | solution.py:62
  143.3 13.8 %collective-permute-start.8 = (f32[5,16,1,256]{3,1,2,0:T(8,128)S(1)}, f32[5,16,1,256]{3,1,2,0:T(8,128)S(1)}, u32[]{:S(2)}, u32[]{:S(2)}) collective-permute-start(f32[5,16,1,256]{3,1,2,0:T(8,128)S(1)} %constant_dynamic-update-slice_fusion.10), channel_id=1, source_target_pairs={{0,4},{4,8},{8,12},{12,0},{1,5},{5,9},{9,13},{13,1},{2,6},{6,10},{... | collective-permute-start | bytes 245768 | tf_op jit(solution)/shard_map/ppermute | solution.py:62
  147.2 10.5 %collective-permute-start.9 = (f32[5,16,1,256]{3,2,1,0:T(1,128)S(1)}, f32[5,16,1,256]{3,2,1,0:T(1,128)S(1)}, u32[]{:S(2)}, u32[]{:S(2)}) collective-permute-start(f32[5,16,1,256]{3,2,1,0:T(1,128)S(1)} %constant_dynamic-update-slice_fusion.15), channel_id=1, source_target_pairs={{4,0},{8,4},{12,8},{0,12},{5,1},{9,5},{13,9},{1,13},{6,2},{10,6},{... | collective-permute-start | bytes 245768 | tf_op jit(solution)/shard_map/ppermute | solution.py:63
  150.6 38.5 %copy-start.6 = (f32[3,2,16,256]{3,2,1,0:T(8,128)}, f32[3,2,16,256]{3,2,1,0:T(8,128)S(1)}, u32[]{:S(2)}) copy-start(f32[3,2,16,256]{3,2,1,0:T(8,128)S(1)} %collective-permute-done.12) | copy-start | bytes 294916
  150.6 21.3 %copy-start.8 = (f32[3,2,16,256]{3,2,1,0:T(8,128)}, f32[3,2,16,256]{3,2,1,0:T(8,128)S(1)}, u32[]{:S(2)}) copy-start(f32[3,2,16,256]{3,2,1,0:T(8,128)S(1)} %collective-permute-done.13) | copy-start | bytes 294916
  151.4 37.7 %collective-permute-start.14 = (f32[3,20,2,256]{3,2,1,0:T(2,128)}, f32[3,20,2,256]{3,2,1,0:T(2,128)}, u32[]{:S(2)}, u32[]{:S(2)}) collective-permute-start(f32[3,20,2,256]{3,2,1,0:T(2,128)} %get-tuple-element.35), channel_id=1, source_target_pairs={{0,4},{4,8},{8,12},{12,0},{1,5},{5,9},{9,13},{13,1},{2,6},{6,10},{... | collective-permute-start | bytes 368648 | tf_op jit(solution)/shard_map/ppermute | solution.py:46
  157.0 32.1 %collective-permute-start.15 = (f32[3,20,2,256]{3,2,1,0:T(2,128)}, f32[3,20,2,256]{3,2,1,0:T(2,128)}, u32[]{:S(2)}, u32[]{:S(2)}) collective-permute-start(f32[3,20,2,256]{3,2,1,0:T(2,128)} %get-tuple-element.36), channel_id=1, source_target_pairs={{4,0},{8,4},{12,8},{0,12},{5,1},{9,5},{13,9},{1,13},{6,2},{10,6},{... | collective-permute-start | bytes 368648 | tf_op jit(solution)/shard_map/ppermute | solution.py:48
  157.1 0.6 copy-start.14
  158.3 13.6 %copy-start.10 = (f32[16,1,256]{2,1,0:T(1,128)}, f32[16,1,256]{2,1,0:T(1,128)S(1)}, u32[]{:S(2)}) copy-start(f32[16,1,256]{2,1,0:T(1,128)S(1)} %get-tuple-element.51) | copy-start | bytes 49156
  158.3 13.6 %copy-start.12 = (f32[16,1,256]{2,1,0:T(1,128)}, f32[16,1,256]{2,1,0:T(1,128)S(1)}, u32[]{:S(2)}) copy-start(f32[16,1,256]{2,1,0:T(1,128)S(1)} %get-tuple-element.50) | copy-start | bytes 49156
  158.4 5.9 %collective-permute-start.11 = (f32[5,16,16,1]{2,1,3,0:T(8,128)S(1)}, f32[5,16,16,1]{2,1,3,0:T(8,128)S(1)}, u32[]{:S(2)}, u32[]{:S(2)}) collective-permute-start(f32[5,16,16,1]{2,1,3,0:T(8,128)S(1)} %constant_dynamic-update-slice_fusion.25), channel_id=1, source_target_pairs={{1,0},{2,1},{3,2},{0,3},{5,4},{6,5},{7,6},{4,7},{9,8},{10,9},{11,1... | collective-permute-start | bytes 15368 | tf_op jit(solution)/shard_map/ppermute | solution.py:63
  159.5 11.5 %copy-start.16 = (f32[16,1,256]{2,1,0:T(1,128)}, f32[16,1,256]{2,1,0:T(1,128)S(1)}, u32[]{:S(2)}) copy-start(f32[16,1,256]{2,1,0:T(1,128)S(1)} %copy.2980) | copy-start | bytes 49156
  161.1 6.1 %collective-permute-start.10 = (f32[5,16,16,1]{2,1,3,0:T(8,128)}, f32[5,16,16,1]{2,1,3,0:T(8,128)}, u32[]{:S(2)}, u32[]{:S(2)}) collective-permute-start(f32[5,16,16,1]{2,1,3,0:T(8,128)} %constant_dynamic-update-slice_fusion.20), channel_id=1, source_target_pairs={{0,1},{1,2},{2,3},{3,0},{4,5},{5,6},{6,7},{7,4},{8,9},{9,10},{10,1... | collective-permute-start | bytes 15368 | tf_op jit(solution)/shard_map/ppermute | solution.py:62
  172.7 10.0 %copy-start.5 = (f32[16,16,1]{2,1,0:T(8,128)S(1)}, f32[16,16,1]{2,1,0:T(8,128)}, u32[]{:S(2)}) copy-start(f32[16,16,1]{2,1,0:T(8,128)} %copy.2986) | copy-start | bytes 3076
  172.7 11.8 %copy-start.4 = (f32[16,16,1]{2,1,0:T(8,128)S(1)}, f32[16,16,1]{2,1,0:T(8,128)}, u32[]{:S(2)}) copy-start(f32[16,16,1]{2,1,0:T(8,128)} %copy.2987) | copy-start | bytes 3076
  178.1 9.0 %copy-start.30 = (f32[16,16,1]{1,0,2:T(8,128)S(1)}, f32[16,16,1]{1,0,2:T(8,128)}, u32[]{:S(2)}) copy-start(f32[16,16,1]{1,0,2:T(8,128)} %get-tuple-element.64) | copy-start | bytes 3076
  178.1 9.2 %copy-start.29 = (f32[16,16,1]{1,0,2:T(8,128)S(1)}, f32[16,16,1]{1,0,2:T(8,128)}, u32[]{:S(2)}) copy-start(f32[16,16,1]{1,0,2:T(8,128)} %get-tuple-element.69) | copy-start | bytes 3076
  189.1 6.2 %copy-start.13 = (f32[16,1,256]{2,1,0:T(1,128)S(1)}, f32[16,1,256]{2,1,0:T(1,128)}, u32[]{:S(2)}) copy-start(f32[16,1,256]{2,1,0:T(1,128)} %copy-done.12) | copy-start | bytes 49156
  190.4 5.8 %copy-start.28 = (f32[16,16,1]{1,0,2:T(8,128)S(1)}, f32[16,16,1]{1,0,2:T(8,128)}, u32[]{:S(2)}) copy-start(f32[16,16,1]{1,0,2:T(8,128)} %get-tuple-element.68) | copy-start | bytes 3076
  190.4 7.0 %copy-start.7 = (f32[3,2,16,256]{3,2,1,0:T(8,128)S(1)}, f32[3,2,16,256]{3,2,1,0:T(8,128)}, u32[]{:S(2)}) copy-start(f32[3,2,16,256]{3,2,1,0:T(8,128)} %copy-done.6) | copy-start | bytes 294916
  190.4 6.9 %copy-start.9 = (f32[3,2,16,256]{3,2,1,0:T(8,128)S(1)}, f32[3,2,16,256]{3,2,1,0:T(8,128)}, u32[]{:S(2)}) copy-start(f32[3,2,16,256]{3,2,1,0:T(8,128)} %copy-done.8) | copy-start | bytes 294916
  190.4 6.9 %copy-start.18 = (f32[2048]{0:T(1024)S(1)}, f32[2048]{0:T(1024)}, u32[]{:S(2)}) copy-start(f32[2048]{0:T(1024)} %copy-done.17) | copy-start | bytes 24580
  190.4 6.9 %copy-start.20 = (f32[2048]{0:T(1024)S(1)}, f32[2048]{0:T(1024)}, u32[]{:S(2)}) copy-start(f32[2048]{0:T(1024)} %copy-done.19) | copy-start | bytes 24580
  190.4 6.9 %copy-start.22 = (f32[2048]{0:T(1024)S(1)}, f32[2048]{0:T(1024)}, u32[]{:S(2)}) copy-start(f32[2048]{0:T(1024)} %copy-done.21) | copy-start | bytes 24580
  191.1 5.2 %collective-permute-start.16 = (f32[3,20,20,2]{2,3,1,0:T(2,128)S(1)}, f32[3,20,20,2]{2,3,1,0:T(2,128)S(1)}, u32[]{:S(2)}, u32[]{:S(2)}) collective-permute-start(f32[3,20,20,2]{2,3,1,0:T(2,128)S(1)} %copy.2994), channel_id=1, source_target_pairs={{0,1},{1,2},{2,3},{3,0},{4,5},{5,6},{6,7},{7,4},{8,9},{9,10},{10,1... | collective-permute-start | bytes 28808 | tf_op jit(solution)/shard_map/ppermute | solution.py:46
  191.7 5.1 %collective-permute-start.17 = (f32[3,20,20,2]{2,3,1,0:T(2,128)S(1)}, f32[3,20,20,2]{2,3,1,0:T(2,128)S(1)}, u32[]{:S(2)}, u32[]{:S(2)}) collective-permute-start(f32[3,20,20,2]{2,3,1,0:T(2,128)S(1)} %copy.2995), channel_id=1, source_target_pairs={{1,0},{2,1},{3,2},{0,3},{5,4},{6,5},{7,6},{4,7},{9,8},{10,9},{11,1... | collective-permute-start | bytes 28808 | tf_op jit(solution)/shard_map/ppermute | solution.py:48
  197.4 28.6 %copy-start.15 = (f32[16,1,256]{2,1,0:T(1,128)S(1)}, f32[16,1,256]{2,1,0:T(1,128)}, u32[]{:S(2)}) copy-start(f32[16,1,256]{2,1,0:T(1,128)} %copy-done.14) | copy-start | bytes 49156
  197.4 29.5 %copy-start.27 = (f32[16,16,1]{1,0,2:T(8,128)S(1)}, f32[16,16,1]{1,0,2:T(8,128)}, u32[]{:S(2)}) copy-start(f32[16,16,1]{1,0,2:T(8,128)} %get-tuple-element.63) | copy-start | bytes 3076
  197.4 41.1 %copy-start.11 = (f32[16,1,256]{2,1,0:T(1,128)S(1)}, f32[16,1,256]{2,1,0:T(1,128)}, u32[]{:S(2)}) copy-start(f32[16,1,256]{2,1,0:T(1,128)} %copy-done.10) | copy-start | bytes 49156
  212.5 33.6 %copy-start.32 = (s32[1024,1]{0,1:T(1,128)S(1)}, s32[1024,1]{0,1:T(1,128)}, u32[]{:S(2)}) copy-start(s32[1024,1]{0,1:T(1,128)} %copy-done.31) | copy-start | bytes 12292
  213.7 19.6 %all-to-all-start.2 = ((f32[16,1,384]{2,1,0:T(1,128)}), f32[16,1,384]{2,1,0:T(1,128)S(1)}, u32[]{:S(2)}, u32[]{:S(2)}) async-start(f32[16,1,384]{2,1,0:T(1,128)} %reshape.859), calls=%async_computation.2 | async-start | bytes 49152 | tf_op jit(solution)/shard_map/all_to_all | solution.py:252
  235.0 9.9 %all-to-all-start.3 = ((f32[16,1,384]{2,1,0:T(1,128)}), f32[16,1,384]{2,1,0:T(1,128)S(1)}, u32[]{:S(2)}, u32[]{:S(2)}) async-start(f32[16,1,384]{2,1,0:T(1,128)} %reshape.861), calls=%async_computation.3 | async-start | bytes 49152 | tf_op jit(solution)/shard_map/all_to_all | solution.py:251
